TPU v7x, 128 devices: a whole 4x4x4 slice. The times are simulated.
128 devices in a mesh: seq: 16 (over y, x), emb: 8 (over z, core).
Axes of the slice: x: 4, y: 4, z: 4, core: 2. Of those that a mesh axis runs over, the one named last changes fastest.
Arguments:
- source: bfloat16 [32768, 1024], P('seq', 'emb'), may hold values from -6 to 6
- target: bfloat16 [32768, 1024], P('seq', 'emb'), may hold values from -6 to 6
- doc_ids: int32 [32768], replicated, may hold values from 0 to 511, never falling along the last dimension, each value on 1 to 512 neighbouring positions
- offsets: int32 [512], P(('seq', 'emb')), may hold values from -2048 to 2048, as said below
Outputs:
- projected: bfloat16 [32768, 1024], P('seq', 'emb')
- row_mass: float32 [32768], P(('seq', 'emb'))
Inputs may be any that keep to these rules, and one draw needn't show every extreme that they name: doc_ids never fall along the sentences. `offsets`: both ends of the range occur in every draw.
All inputs are finite; a program needn't handle non-finite values.
Results may differ from a plain program's by a relative error of at most 0.006.
Values may be sent and summed in bfloat16 or wider, within the bound.
No kernel may reach another device: no remote copies, remote signals or barrier semaphores. Data moves between devices by JAX's collectives and lax.ppermute only.
A program may use at most 128 MiB of HBM per device.

v0:
```python
import jax
import jax.numpy as jnp
from jax import lax
from jax.sharding import PartitionSpec as P

BAND = 2048
OFFSET_BLOCK = 64
ITERS = 3


INV_EPS = 50.0
PENALTY = 0.04


def shifted_2(block, axis, distance):
    devices = range(lax.axis_size(axis))
    route = [(i - distance, i) for i in devices if i - distance in devices]
    return lax.ppermute(block, axis, route)


def per_device(source, target, doc_ids, offsets):
    n_emb = lax.axis_size("emb")
    rows_dev = source.shape[0] // n_emb
    place = lax.axis_index(("seq", "emb"))
    sentences = doc_ids.shape[0]
    reach = 2 * BAND
    hops = reach // rows_dev
    width = rows_dev + 2 * reach
    src_rows, tgt_rows = (
        lax.all_to_all(source, "emb", split_axis=0, concat_axis=1, tiled=True),
        lax.all_to_all(target, "emb", split_axis=0, concat_axis=1, tiled=True),
    )
    lower = {}
    upper = {}
    for dist in range(1, hops + 1):
        for sign in (1, -1):
            moved = shifted_2(tgt_rows, ("seq", "emb"), -sign * dist)
            if sign > 0:
                upper[dist] = moved
            else:
                lower[dist] = moved
    pieces = (
        [lower[dist] for dist in range(hops, 0, -1)]
        + [tgt_rows]
        + [upper[dist] for dist in range(1, hops + 1)]
    )
    window = jnp.concatenate(pieces, axis=0)
    src_scale = lax.rsqrt(jnp.sum(jnp.square(src_rows.astype(jnp.float32)), axis=1) + 1e-06)
    tgt_scale = lax.rsqrt(jnp.sum(jnp.square(window.astype(jnp.float32)), axis=1) + 1e-06)
    first_row = place * rows_dev
    src_pos = first_row + jnp.arange(rows_dev, dtype=jnp.int32)
    tgt_pos = first_row - reach + jnp.arange(width, dtype=jnp.int32)
    valid = (tgt_pos >= 0) & (tgt_pos < sentences)
    shifted = jnp.repeat(offsets, OFFSET_BLOCK)
    band = (jnp.abs(tgt_pos[None, :] - src_pos[:, None] - shifted[:, None]) <= BAND) & valid[
        None, :
    ]
    pad_docs = jnp.pad(doc_ids, (reach, reach), constant_values=-1)
    same = (
        lax.dynamic_slice_in_dim(doc_ids, first_row, rows_dev, 0)[:, None]
        == lax.dynamic_slice_in_dim(pad_docs, first_row, width, 0)[None, :]
    )
    penalty = jnp.where(same, 0.0, PENALTY)

    def cosines():
        dots = lax.dot_general(
            src_rows, window, (((1,), (1,)), ((), ())), preferred_element_type=jnp.float32
        )
        return dots * src_scale[:, None] * tgt_scale[None, :]

    def to_kernel(cosine):
        return jnp.where(band, jnp.exp((cosine - penalty) * INV_EPS), 0.0)

    def kernel():
        return to_kernel(cosines())

    scaling = valid.astype(jnp.float32)
    inverse = jnp.zeros((rows_dev,), jnp.float32)
    for step in range(ITERS):
        kern = kernel()
        inverse = 1.0 / jnp.sum(kern * scaling[None, :], axis=1)
        part = jnp.sum(kern * inverse[:, None], axis=0)
        owned = part[reach : reach + rows_dev]
        for lag in range(-hops, hops + 1):
            if lag != 0:
                begin = reach + lag * rows_dev
                owned = owned + shifted_2(part[begin : begin + rows_dev], ("seq", "emb"), lag)
        own_scaling = 1.0 / owned
        parts_list = []
        for lag in range(-hops, hops + 1):
            if lag == 0:
                parts_list.append(own_scaling)
            else:
                parts_list.append(shifted_2(own_scaling, ("seq", "emb"), -lag))
        scaling = jnp.concatenate(parts_list, axis=0)
    kern = kernel()
    totals = jnp.sum(kern * scaling[None, :], axis=1)
    row_mass = inverse * totals
    weights = (kern * scaling[None, :] / totals[:, None]).astype(jnp.bfloat16)
    mixed = jnp.dot(weights, window, preferred_element_type=jnp.float32).astype(jnp.bfloat16)
    projected = lax.all_to_all(mixed, "emb", split_axis=1, concat_axis=0, tiled=True)
    return (projected, row_mass)


def solution(mesh):
    in_specs = (P("seq", "emb"), P("seq", "emb"), P(), P(("seq", "emb")))
    out_specs = (P("seq", "emb"), P(("seq", "emb")))
    return jax.shard_map(
        per_device, mesh=mesh, in_specs=in_specs, out_specs=out_specs, check_vma=False
    )
```

profile of v0, /device:TPU:26, one launch (start us, length us, event | category | flops | bytes accessed | tf_op | source)
XLA Modules:
  0.0 1185.0 jit_solution(1523903914332999481)
XLA Ops:
  6.0 10.3 all-to-all-done
  43.1 11.2 collective-permute-done.1
  56.2 10.9 collective-permute-done.2
  70.1 8.2 collective-permute-done.3
  80.3 9.3 collective-permute-done.4
  91.5 9.4 collective-permute-done.5
  102.9 9.3 collective-permute-done.6
  114.1 9.3 collective-permute-done.7
  126.7 7.9 collective-permute-done.8
  136.6 12.5 %collective-permute-start.14 = (bf16[256,1024]{0,1:T(8,128)(2,1)S(1)}, bf16[256,1024]{0,1:T(8,128)(2,1)S(1)}, u32[]{:S(2)}, u32[]{:S(2)}) collective-permute-start(bf16[256,1024]{0,1:T(8,128)(2,1)S(1)} %bitcast.43), channel_id=1, source_target_pairs={{0,2},{1,3},{2,4},{3,5},{4,6},{5,7},{6,8},{7,9},{8,10},{9,11},{10,... | collective-permute-start | bytes 1572872 | tf_op jit(solution)/shard_map/ppermute | solution.py:18
  158.7 6.5 collective-permute-start.16
  165.3 13.0 %collective-permute-done.12 = bf16[256,1024]{0,1:T(8,128)(2,1)S(1)} collective-permute-done((bf16[256,1024]{0,1:T(8,128)(2,1)S(1)}, bf16[256,1024]{0,1:T(8,128)(2,1)S(1)}, u32[]{:S(2)}, u32[]{:S(2)}) %collective-permute-start.12) | collective-permute-done | bytes 524320 | tf_op jit(solution)/shard_map/ppermute | solution.py:18
  180.3 6.4 collective-permute-done.13
  188.7 16.5 %collective-permute-done.14 = bf16[256,1024]{0,1:T(8,128)(2,1)S(1)} collective-permute-done((bf16[256,1024]{0,1:T(8,128)(2,1)S(1)}, bf16[256,1024]{0,1:T(8,128)(2,1)S(1)}, u32[]{:S(2)}, u32[]{:S(2)}) %collective-permute-start.14) | collective-permute-done | bytes 524320 | tf_op jit(solution)/shard_map/ppermute | solution.py:18
  207.1 6.8 collective-permute-done.15
  225.8 21.5 %collective-permute-done.19 = bf16[256,1024]{0,1:T(8,128)(2,1)S(1)} collective-permute-done((bf16[256,1024]{0,1:T(8,128)(2,1)S(1)}, bf16[256,1024]{0,1:T(8,128)(2,1)S(1)}, u32[]{:S(2)}, u32[]{:S(2)}) %collective-permute-start.19) | collective-permute-done | bytes 524320 | tf_op jit(solution)/shard_map/ppermute | solution.py:18
  260.9 6.5 collective-permute-done.23
  273.1 17.7 %collective-permute-start.29 = (bf16[256,1024]{0,1:T(8,128)(2,1)S(1)}, bf16[256,1024]{0,1:T(8,128)(2,1)S(1)}, u32[]{:S(2)}, u32[]{:S(2)}) collective-permute-start(bf16[256,1024]{0,1:T(8,128)(2,1)S(1)} %bitcast.59), channel_id=1, source_target_pairs={{14,0},{15,1},{16,2},{17,3},{18,4},{19,5},{20,6},{21,7},{22,8},{23... | collective-permute-start | bytes 1572872 | tf_op jit(solution)/shard_map/ppermute | solution.py:18
  300.4 60.8 %collective-permute-start.31 = (bf16[256,1024]{0,1:T(8,128)(2,1)S(1)}, bf16[256,1024]{0,1:T(8,128)(2,1)S(1)}, u32[]{:S(2)}, u32[]{:S(2)}) collective-permute-start(bf16[256,1024]{0,1:T(8,128)(2,1)S(1)} %bitcast.61), channel_id=1, source_target_pairs={{16,0},{17,1},{18,2},{19,3},{20,4},{21,5},{22,6},{23,7},{24,8},{25... | collective-permute-start | bytes 1572872 | tf_op jit(solution)/shard_map/ppermute | solution.py:18
  361.5 34.7 %collective-permute-done.31 = bf16[256,1024]{0,1:T(8,128)(2,1)S(1)} collective-permute-done((bf16[256,1024]{0,1:T(8,128)(2,1)S(1)}, bf16[256,1024]{0,1:T(8,128)(2,1)S(1)}, u32[]{:S(2)}, u32[]{:S(2)}) %collective-permute-start.31) | collective-permute-done | bytes 524320 | tf_op jit(solution)/shard_map/ppermute | solution.py:18
  400.6 11.5 multiply_reduce_fusion.6
  432.5 6.5 collective-permute-start.51
  465.4 6.8 collective-permute-start.33
  472.2 6.5 collective-permute-start.34
  478.7 8.5 collective-permute-start.35
  487.2 6.9 collective-permute-start.36
  499.0 8.1 collective-permute-start.38
  582.5 8.9 collective-permute-start.83
  593.7 6.0 collective-permute-start.85
  608.4 7.8 collective-permute-start.88
  626.6 9.1 collective-permute-start.91
  709.2 6.7 collective-permute-start.96
  715.8 7.8 collective-permute-start.100
  728.7 8.0 collective-permute-start.102
  830.3 9.0 collective-permute-start.147
  855.3 8.1 collective-permute-start.152
  866.8 6.7 collective-permute-start.154
  873.5 8.7 collective-permute-start.155
  961.3 7.3 collective-permute-start.161
  968.6 6.0 collective-permute-start.162
  974.7 8.4 collective-permute-start.163
  983.1 6.9 collective-permute-start.164
  995.0 8.1 collective-permute-start.166
  1078.4 8.8 collective-permute-start.211
  1104.3 7.8 collective-permute-start.216
  1122.5 9.1 collective-permute-start.219
  1156.0 12.8 %fusion.11 = bf16[32,8,8,128]{3,2,1,0:T(8,128)(2,1)S(1)} fusion(bf16[8448,1024]{0,1:T(8,128)(2,1)} %copy-done.1, f32[256,8448]{0,1:T(8,128)} %copy-done, f32[256]{0:T(256)S(1)} %multiply_reduce_fusion.7, f32[8448]{0:T(1024)S(1)} %constant_dynamic-update-slice_fusion.38), kind=kOutput, calls=%fused_computation.22 | convolution fusion | flops 4435935232 | bytes 26511360 | tf_op jit(solution)/shard_map/dot_general | solution.py:100
  1174.2 9.7 all-to-all-done.2
  (580 shorter events, 664.5 us)
Async XLA Ops:
  24.9 29.3 %collective-permute-start.1 = (bf16[256,1024]{0,1:T(8,128)(2,1)S(1)}, bf16[256,1024]{0,1:T(8,128)(2,1)S(1)}, u32[]{:S(2)}, u32[]{:S(2)}) collective-permute-start(bf16[256,1024]{0,1:T(8,128)(2,1)S(1)} %bitcast.30), channel_id=1, source_target_pairs={{0,15},{1,16},{2,17},{3,18},{4,19},{5,20},{6,21},{7,22},{8,23},{9,... | collective-permute-start | bytes 1572872 | tf_op jit(solution)/shard_map/ppermute | solution.py:18
  29.5 37.6 %collective-permute-start.2 = (bf16[256,1024]{0,1:T(8,128)(2,1)S(1)}, bf16[256,1024]{0,1:T(8,128)(2,1)}, u32[]{:S(2)}, u32[]{:S(2)}) collective-permute-start(bf16[256,1024]{0,1:T(8,128)(2,1)S(1)} %bitcast.31), channel_id=1, source_target_pairs={{0,14},{1,15},{2,16},{3,17},{4,18},{5,19},{6,20},{7,21},{8,22},{9,... | collective-permute-start | bytes 1572872 | tf_op jit(solution)/shard_map/ppermute | solution.py:18
  31.4 46.9 %collective-permute-start.3 = (bf16[256,1024]{0,1:T(8,128)(2,1)S(1)}, bf16[256,1024]{0,1:T(8,128)(2,1)S(1)}, u32[]{:S(2)}, u32[]{:S(2)}) collective-permute-start(bf16[256,1024]{0,1:T(8,128)(2,1)S(1)} %bitcast.32), channel_id=1, source_target_pairs={{0,13},{1,14},{2,15},{3,16},{4,17},{5,18},{6,19},{7,20},{8,21},{9,... | collective-permute-start | bytes 1572872 | tf_op jit(solution)/shard_map/ppermute | solution.py:18
  33.3 56.2 %collective-permute-start.4 = (bf16[256,1024]{0,1:T(8,128)(2,1)S(1)}, bf16[256,1024]{0,1:T(8,128)(2,1)S(1)}, u32[]{:S(2)}, u32[]{:S(2)}) collective-permute-start(bf16[256,1024]{0,1:T(8,128)(2,1)S(1)} %bitcast.33), channel_id=1, source_target_pairs={{0,12},{1,13},{2,14},{3,15},{4,16},{5,17},{6,18},{7,19},{8,20},{9,... | collective-permute-start | bytes 1572872 | tf_op jit(solution)/shard_map/ppermute | solution.py:18
  40.1 60.9 %collective-permute-start.5 = (bf16[256,1024]{0,1:T(8,128)(2,1)S(1)}, bf16[256,1024]{0,1:T(8,128)(2,1)S(1)}, u32[]{:S(2)}, u32[]{:S(2)}) collective-permute-start(bf16[256,1024]{0,1:T(8,128)(2,1)S(1)} %bitcast.34), channel_id=1, source_target_pairs={{0,11},{1,12},{2,13},{3,14},{4,15},{5,16},{6,17},{7,18},{8,19},{9,... | collective-permute-start | bytes 1572872 | tf_op jit(solution)/shard_map/ppermute | solution.py:18
  54.2 57.9 %collective-permute-start.6 = (bf16[256,1024]{0,1:T(8,128)(2,1)S(1)}, bf16[256,1024]{0,1:T(8,128)(2,1)S(1)}, u32[]{:S(2)}, u32[]{:S(2)}) collective-permute-start(bf16[256,1024]{0,1:T(8,128)(2,1)S(1)} %bitcast.35), channel_id=1, source_target_pairs={{0,10},{1,11},{2,12},{3,13},{4,14},{5,15},{6,16},{7,17},{8,18},{9,... | collective-permute-start | bytes 1572872 | tf_op jit(solution)/shard_map/ppermute | solution.py:18
  67.1 56.3 %collective-permute-start.7 = (bf16[256,1024]{0,1:T(8,128)(2,1)S(1)}, bf16[256,1024]{0,1:T(8,128)(2,1)S(1)}, u32[]{:S(2)}, u32[]{:S(2)}) collective-permute-start(bf16[256,1024]{0,1:T(8,128)(2,1)S(1)} %bitcast.36), channel_id=1, source_target_pairs={{0,9},{1,10},{2,11},{3,12},{4,13},{5,14},{6,15},{7,16},{8,17},{9,1... | collective-permute-start | bytes 1572872 | tf_op jit(solution)/shard_map/ppermute | solution.py:18
  78.3 56.3 %collective-permute-start.8 = (bf16[256,1024]{0,1:T(8,128)(2,1)S(1)}, bf16[256,1024]{0,1:T(8,128)(2,1)S(1)}, u32[]{:S(2)}, u32[]{:S(2)}) collective-permute-start(bf16[256,1024]{0,1:T(8,128)(2,1)S(1)} %bitcast.37), channel_id=1, source_target_pairs={{0,8},{1,9},{2,10},{3,11},{4,12},{5,13},{6,14},{7,15},{8,16},{9,17... | collective-permute-start | bytes 1572872 | tf_op jit(solution)/shard_map/ppermute | solution.py:18
  89.5 47.1 %collective-permute-start.9 = (bf16[256,1024]{0,1:T(8,128)(2,1)S(1)}, bf16[256,1024]{0,1:T(8,128)(2,1)S(1)}, u32[]{:S(2)}, u32[]{:S(2)}) collective-permute-start(bf16[256,1024]{0,1:T(8,128)(2,1)S(1)} %bitcast.38), channel_id=1, source_target_pairs={{0,7},{1,8},{2,9},{3,10},{4,11},{5,12},{6,13},{7,14},{8,15},{9,16}... | collective-permute-start | bytes 1572872 | tf_op jit(solution)/shard_map/ppermute | solution.py:18
  100.9 53.0 %collective-permute-start.10 = (bf16[256,1024]{0,1:T(8,128)(2,1)S(1)}, bf16[256,1024]{0,1:T(8,128)(2,1)S(1)}, u32[]{:S(2)}, u32[]{:S(2)}) collective-permute-start(bf16[256,1024]{0,1:T(8,128)(2,1)S(1)} %bitcast.39), channel_id=1, source_target_pairs={{0,6},{1,7},{2,8},{3,9},{4,10},{5,11},{6,12},{7,13},{8,14},{9,15},... | collective-permute-start | bytes 1572872 | tf_op jit(solution)/shard_map/ppermute | solution.py:18
  112.2 46.5 %collective-permute-start.11 = (bf16[256,1024]{0,1:T(8,128)(2,1)S(1)}, bf16[256,1024]{0,1:T(8,128)(2,1)S(1)}, u32[]{:S(2)}, u32[]{:S(2)}) collective-permute-start(bf16[256,1024]{0,1:T(8,128)(2,1)S(1)} %bitcast.40), channel_id=1, source_target_pairs={{0,5},{1,6},{2,7},{3,8},{4,9},{5,10},{6,11},{7,12},{8,13},{9,14},{... | collective-permute-start | bytes 1572872 | tf_op jit(solution)/shard_map/ppermute | solution.py:18
  123.4 54.9 %collective-permute-start.12 = (bf16[256,1024]{0,1:T(8,128)(2,1)S(1)}, bf16[256,1024]{0,1:T(8,128)(2,1)S(1)}, u32[]{:S(2)}, u32[]{:S(2)}) collective-permute-start(bf16[256,1024]{0,1:T(8,128)(2,1)S(1)} %bitcast.41), channel_id=1, source_target_pairs={{0,4},{1,5},{2,6},{3,7},{4,8},{5,9},{6,10},{7,11},{8,12},{9,13},{1... | collective-permute-start | bytes 1572872 | tf_op jit(solution)/shard_map/ppermute | solution.py:18
  134.6 52.1 %collective-permute-start.13 = (bf16[256,1024]{0,1:T(8,128)(2,1)S(1)}, bf16[256,1024]{0,1:T(8,128)(2,1)S(1)}, u32[]{:S(2)}, u32[]{:S(2)}) collective-permute-start(bf16[256,1024]{0,1:T(8,128)(2,1)S(1)} %bitcast.42), channel_id=1, source_target_pairs={{0,3},{1,4},{2,5},{3,6},{4,7},{5,8},{6,9},{7,10},{8,11},{9,12},{10... | collective-permute-start | bytes 1572872 | tf_op jit(solution)/shard_map/ppermute | solution.py:18
  136.6 68.6 %collective-permute-start.14 = (bf16[256,1024]{0,1:T(8,128)(2,1)S(1)}, bf16[256,1024]{0,1:T(8,128)(2,1)S(1)}, u32[]{:S(2)}, u32[]{:S(2)}) collective-permute-start(bf16[256,1024]{0,1:T(8,128)(2,1)S(1)} %bitcast.43), channel_id=1, source_target_pairs={{0,2},{1,3},{2,4},{3,5},{4,6},{5,7},{6,8},{7,9},{8,10},{9,11},{10,... | collective-permute-start | bytes 1572872 | tf_op jit(solution)/shard_map/ppermute | solution.py:18
  153.9 60.1 %collective-permute-start.15 = (bf16[256,1024]{0,1:T(8,128)(2,1)S(1)}, bf16[256,1024]{0,1:T(8,128)(2,1)S(1)}, u32[]{:S(2)}, u32[]{:S(2)}) collective-permute-start(bf16[256,1024]{0,1:T(8,128)(2,1)S(1)} %bitcast.44), channel_id=1, source_target_pairs={{0,1},{1,2},{2,3},{3,4},{4,5},{5,6},{6,7},{7,8},{8,9},{9,10},{10,1... | collective-permute-start | bytes 1572872 | tf_op jit(solution)/shard_map/ppermute | solution.py:18
  158.7 57.3 %collective-permute-start.16 = (bf16[256,1024]{0,1:T(8,128)(2,1)S(1)}, bf16[256,1024]{0,1:T(8,128)(2,1)S(1)}, u32[]{:S(2)}, u32[]{:S(2)}) collective-permute-start(bf16[256,1024]{0,1:T(8,128)(2,1)S(1)} %bitcast.45), channel_id=1, source_target_pairs={{1,0},{2,1},{3,2},{4,3},{5,4},{6,5},{7,6},{8,7},{9,8},{10,9},{11,1... | collective-permute-start | bytes 1572872 | tf_op jit(solution)/shard_map/ppermute | solution.py:18
  178.3 39.7 %collective-permute-start.17 = (bf16[256,1024]{0,1:T(8,128)(2,1)S(1)}, bf16[256,1024]{0,1:T(8,128)(2,1)S(1)}, u32[]{:S(2)}, u32[]{:S(2)}) collective-permute-start(bf16[256,1024]{0,1:T(8,128)(2,1)S(1)} %bitcast.46), channel_id=1, source_target_pairs={{2,0},{3,1},{4,2},{5,3},{6,4},{7,5},{8,6},{9,7},{10,8},{11,9},{12,... | collective-permute-start | bytes 1572872 | tf_op jit(solution)/shard_map/ppermute | solution.py:18
  186.7 33.3 %collective-permute-start.18 = (bf16[256,1024]{0,1:T(8,128)(2,1)S(1)}, bf16[256,1024]{0,1:T(8,128)(2,1)S(1)}, u32[]{:S(2)}, u32[]{:S(2)}) collective-permute-start(bf16[256,1024]{0,1:T(8,128)(2,1)S(1)} %bitcast.47), channel_id=1, source_target_pairs={{3,0},{4,1},{5,2},{6,3},{7,4},{8,5},{9,6},{10,7},{11,8},{12,9},{13... | collective-permute-start | bytes 1572872 | tf_op jit(solution)/shard_map/ppermute | solution.py:18
  205.2 42.1 %collective-permute-start.19 = (bf16[256,1024]{0,1:T(8,128)(2,1)S(1)}, bf16[256,1024]{0,1:T(8,128)(2,1)S(1)}, u32[]{:S(2)}, u32[]{:S(2)}) collective-permute-start(bf16[256,1024]{0,1:T(8,128)(2,1)S(1)} %bitcast.48), channel_id=1, source_target_pairs={{4,0},{5,1},{6,2},{7,3},{8,4},{9,5},{10,6},{11,7},{12,8},{13,9},{1... | collective-permute-start | bytes 1572872 | tf_op jit(solution)/shard_map/ppermute | solution.py:18
  214.0 36.2 %collective-permute-start.20 = (bf16[256,1024]{0,1:T(8,128)(2,1)S(1)}, bf16[256,1024]{0,1:T(8,128)(2,1)S(1)}, u32[]{:S(2)}, u32[]{:S(2)}) collective-permute-start(bf16[256,1024]{0,1:T(8,128)(2,1)S(1)} %bitcast.49), channel_id=1, source_target_pairs={{5,0},{6,1},{7,2},{8,3},{9,4},{10,5},{11,6},{12,7},{13,8},{14,9},{... | collective-permute-start | bytes 1572872 | tf_op jit(solution)/shard_map/ppermute | solution.py:18
  216.0 36.2 %collective-permute-start.21 = (bf16[256,1024]{0,1:T(8,128)(2,1)S(1)}, bf16[256,1024]{0,1:T(8,128)(2,1)S(1)}, u32[]{:S(2)}, u32[]{:S(2)}) collective-permute-start(bf16[256,1024]{0,1:T(8,128)(2,1)S(1)} %bitcast.51), channel_id=1, source_target_pairs={{6,0},{7,1},{8,2},{9,3},{10,4},{11,5},{12,6},{13,7},{14,8},{15,9},... | collective-permute-start | bytes 1572872 | tf_op jit(solution)/shard_map/ppermute | solution.py:18
  218.0 38.3 %collective-permute-start.22 = (bf16[256,1024]{0,1:T(8,128)(2,1)S(1)}, bf16[256,1024]{0,1:T(8,128)(2,1)S(1)}, u32[]{:S(2)}, u32[]{:S(2)}) collective-permute-start(bf16[256,1024]{0,1:T(8,128)(2,1)S(1)} %bitcast.52), channel_id=1, source_target_pairs={{7,0},{8,1},{9,2},{10,3},{11,4},{12,5},{13,6},{14,7},{15,8},{16,9}... | collective-permute-start | bytes 1572872 | tf_op jit(solution)/shard_map/ppermute | solution.py:18
  220.0 47.5 %collective-permute-start.23 = (bf16[256,1024]{0,1:T(8,128)(2,1)S(1)}, bf16[256,1024]{0,1:T(8,128)(2,1)S(1)}, u32[]{:S(2)}, u32[]{:S(2)}) collective-permute-start(bf16[256,1024]{0,1:T(8,128)(2,1)S(1)} %bitcast.53), channel_id=1, source_target_pairs={{8,0},{9,1},{10,2},{11,3},{12,4},{13,5},{14,6},{15,7},{16,8},{17,9... | collective-permute-start | bytes 1572872 | tf_op jit(solution)/shard_map/ppermute | solution.py:18
  250.2 45.4 %collective-permute-start.25 = (bf16[256,1024]{0,1:T(8,128)(2,1)S(1)}, bf16[256,1024]{0,1:T(8,128)(2,1)S(1)}, u32[]{:S(2)}, u32[]{:S(2)}) collective-permute-start(bf16[256,1024]{0,1:T(8,128)(2,1)S(1)} %bitcast.55), channel_id=1, source_target_pairs={{10,0},{11,1},{12,2},{13,3},{14,4},{15,5},{16,6},{17,7},{18,8},{19... | collective-permute-start | bytes 1572872 | tf_op jit(solution)/shard_map/ppermute | solution.py:18
  252.2 48.2 %collective-permute-start.26 = (bf16[256,1024]{0,1:T(8,128)(2,1)S(1)}, bf16[256,1024]{0,1:T(8,128)(2,1)S(1)}, u32[]{:S(2)}, u32[]{:S(2)}) collective-permute-start(bf16[256,1024]{0,1:T(8,128)(2,1)S(1)} %bitcast.56), channel_id=1, source_target_pairs={{11,0},{12,1},{13,2},{14,3},{15,4},{16,5},{17,6},{18,7},{19,8},{20... | collective-permute-start | bytes 1572872 | tf_op jit(solution)/shard_map/ppermute | solution.py:18
  256.3 105.0 %collective-permute-start.27 = (bf16[256,1024]{0,1:T(8,128)(2,1)S(1)}, bf16[256,1024]{0,1:T(8,128)(2,1)S(1)}, u32[]{:S(2)}, u32[]{:S(2)}) collective-permute-start(bf16[256,1024]{0,1:T(8,128)(2,1)S(1)} %bitcast.57), channel_id=1, source_target_pairs={{12,0},{13,1},{14,2},{15,3},{16,4},{17,5},{18,6},{19,7},{20,8},{21... | collective-permute-start | bytes 1572872 | tf_op jit(solution)/shard_map/ppermute | solution.py:18
  267.4 93.9 %collective-permute-start.28 = (bf16[256,1024]{0,1:T(8,128)(2,1)S(1)}, bf16[256,1024]{0,1:T(8,128)(2,1)S(1)}, u32[]{:S(2)}, u32[]{:S(2)}) collective-permute-start(bf16[256,1024]{0,1:T(8,128)(2,1)S(1)} %bitcast.58), channel_id=1, source_target_pairs={{13,0},{14,1},{15,2},{16,3},{17,4},{18,5},{19,6},{20,7},{21,8},{22... | collective-permute-start | bytes 1572872 | tf_op jit(solution)/shard_map/ppermute | solution.py:18
  273.1 88.3 %collective-permute-start.29 = (bf16[256,1024]{0,1:T(8,128)(2,1)S(1)}, bf16[256,1024]{0,1:T(8,128)(2,1)S(1)}, u32[]{:S(2)}, u32[]{:S(2)}) collective-permute-start(bf16[256,1024]{0,1:T(8,128)(2,1)S(1)} %bitcast.59), channel_id=1, source_target_pairs={{14,0},{15,1},{16,2},{17,3},{18,4},{19,5},{20,6},{21,7},{22,8},{23... | collective-permute-start | bytes 1572872 | tf_op jit(solution)/shard_map/ppermute | solution.py:18
  295.7 65.8 %collective-permute-start.30 = (bf16[256,1024]{0,1:T(8,128)(2,1)S(1)}, bf16[256,1024]{0,1:T(8,128)(2,1)S(1)}, u32[]{:S(2)}, u32[]{:S(2)}) collective-permute-start(bf16[256,1024]{0,1:T(8,128)(2,1)S(1)} %bitcast.60), channel_id=1, source_target_pairs={{15,0},{16,1},{17,2},{18,3},{19,4},{20,5},{21,6},{22,7},{23,8},{24... | collective-permute-start | bytes 1572872 | tf_op jit(solution)/shard_map/ppermute | solution.py:18
  300.4 95.8 %collective-permute-start.31 = (bf16[256,1024]{0,1:T(8,128)(2,1)S(1)}, bf16[256,1024]{0,1:T(8,128)(2,1)S(1)}, u32[]{:S(2)}, u32[]{:S(2)}) collective-permute-start(bf16[256,1024]{0,1:T(8,128)(2,1)S(1)} %bitcast.61), channel_id=1, source_target_pairs={{16,0},{17,1},{18,2},{19,3},{20,4},{21,5},{22,6},{23,7},{24,8},{25... | collective-permute-start | bytes 1572872 | tf_op jit(solution)/shard_map/ppermute | solution.py:18
  463.1 31.0 %collective-permute-start.63 = (f32[256]{0:T(256)S(1)}, f32[256]{0:T(256)S(1)}, u32[]{:S(2)}, u32[]{:S(2)}) collective-permute-start(f32[256]{0:T(256)S(1)} %get-tuple-element.67), channel_id=1, source_target_pairs={{0,16},{1,17},{2,18},{3,19},{4,20},{5,21},{6,22},{7,23},{8,24},{9,... | collective-permute-start | bytes 3080 | tf_op jit(solution)/shard_map/ppermute | solution.py:18
  465.4 33.7 %collective-permute-start.33 = (f32[256]{0:T(256)S(1)}, f32[256]{0:T(256)S(1)}, u32[]{:S(2)}, u32[]{:S(2)}) collective-permute-start(f32[256]{0:T(256)S(1)} %get-tuple-element.85), channel_id=1, source_target_pairs={{15,0},{16,1},{17,2},{18,3},{19,4},{20,5},{21,6},{22,7},{23,8},{24... | collective-permute-start | bytes 3080 | tf_op jit(solution)/shard_map/ppermute | solution.py:18
  472.2 35.0 %collective-permute-start.34 = (f32[256]{0:T(256)S(1)}, f32[256]{0:T(256)S(1)}, u32[]{:S(2)}, u32[]{:S(2)}) collective-permute-start(f32[256]{0:T(256)S(1)} %get-tuple-element.97), channel_id=1, source_target_pairs={{14,0},{15,1},{16,2},{17,3},{18,4},{19,5},{20,6},{21,7},{22,8},{23... | collective-permute-start | bytes 3080 | tf_op jit(solution)/shard_map/ppermute | solution.py:18
  478.7 30.5 %collective-permute-start.35 = (f32[256]{0:T(256)S(1)}, f32[256]{0:T(256)S(1)}, u32[]{:S(2)}, u32[]{:S(2)}) collective-permute-start(f32[256]{0:T(256)S(1)} %get-tuple-element.96), channel_id=1, source_target_pairs={{13,0},{14,1},{15,2},{16,3},{17,4},{18,5},{19,6},{20,7},{21,8},{22... | collective-permute-start | bytes 3080 | tf_op jit(solution)/shard_map/ppermute | solution.py:18
  603.9 31.8 %collective-permute-start.87 = (f32[256]{0:T(256)S(1)}, f32[256]{0:T(256)S(1)}, u32[]{:S(2)}, u32[]{:S(2)}) collective-permute-start(f32[256]{0:T(256)S(1)} %add_divide_fusion.2), channel_id=1, source_target_pairs={{8,0},{9,1},{10,2},{11,3},{12,4},{13,5},{14,6},{15,7},{16,8},{17,9... | collective-permute-start | bytes 3080 | tf_op jit(solution)/shard_map/ppermute | solution.py:18
  608.4 31.2 %collective-permute-start.88 = (f32[256]{0:T(256)S(1)}, f32[256]{0:T(256)S(1)}, u32[]{:S(2)}, u32[]{:S(2)}) collective-permute-start(f32[256]{0:T(256)S(1)} %add_divide_fusion.2), channel_id=1, source_target_pairs={{9,0},{10,1},{11,2},{12,3},{13,4},{14,5},{15,6},{16,7},{17,8},{18,... | collective-permute-start | bytes 3080 | tf_op jit(solution)/shard_map/ppermute | solution.py:18
  616.3 28.6 %collective-permute-start.89 = (f32[256]{0:T(256)S(1)}, f32[256]{0:T(256)S(1)}, u32[]{:S(2)}, u32[]{:S(2)}) collective-permute-start(f32[256]{0:T(256)S(1)} %add_divide_fusion.2), channel_id=1, source_target_pairs={{10,0},{11,1},{12,2},{13,3},{14,4},{15,5},{16,6},{17,7},{18,8},{19... | collective-permute-start | bytes 3080 | tf_op jit(solution)/shard_map/ppermute | solution.py:18
  706.2 30.5 %collective-permute-start.127 = (f32[256]{0:T(256)S(1)}, f32[256]{0:T(256)S(1)}, u32[]{:S(2)}, u32[]{:S(2)}) collective-permute-start(f32[256]{0:T(256)S(1)} %get-tuple-element.35), channel_id=1, source_target_pairs={{0,16},{1,17},{2,18},{3,19},{4,20},{5,21},{6,22},{7,23},{8,24},{9,... | collective-permute-start | bytes 3080 | tf_op jit(solution)/shard_map/ppermute | solution.py:18
  709.2 33.0 %collective-permute-start.96 = (f32[256]{0:T(256)S(1)}, f32[256]{0:T(256)S(1)}, u32[]{:S(2)}, u32[]{:S(2)}) collective-permute-start(f32[256]{0:T(256)S(1)} %get-tuple-element.34), channel_id=1, source_target_pairs={{16,0},{17,1},{18,2},{19,3},{20,4},{21,5},{22,6},{23,7},{24,8},{25... | collective-permute-start | bytes 3080 | tf_op jit(solution)/shard_map/ppermute | solution.py:18
  715.8 31.0 %collective-permute-start.100 = (f32[256]{0:T(256)S(1)}, f32[256]{0:T(256)S(1)}, u32[]{:S(2)}, u32[]{:S(2)}) collective-permute-start(f32[256]{0:T(256)S(1)} %get-tuple-element.63), channel_id=1, source_target_pairs={{12,0},{13,1},{14,2},{15,3},{16,4},{17,5},{18,6},{19,7},{20,8},{21... | collective-permute-start | bytes 3080 | tf_op jit(solution)/shard_map/ppermute | solution.py:18
  851.1 31.2 %collective-permute-start.151 = (f32[256]{0:T(256)S(1)}, f32[256]{0:T(256)S(1)}, u32[]{:S(2)}, u32[]{:S(2)}) collective-permute-start(f32[256]{0:T(256)S(1)} %add_divide_fusion.1), channel_id=1, source_target_pairs={{8,0},{9,1},{10,2},{11,3},{12,4},{13,5},{14,6},{15,7},{16,8},{17,9... | collective-permute-start | bytes 3080 | tf_op jit(solution)/shard_map/ppermute | solution.py:18
  855.3 31.6 %collective-permute-start.152 = (f32[256]{0:T(256)S(1)}, f32[256]{0:T(256)S(1)}, u32[]{:S(2)}, u32[]{:S(2)}) collective-permute-start(f32[256]{0:T(256)S(1)} %add_divide_fusion.1), channel_id=1, source_target_pairs={{9,0},{10,1},{11,2},{12,3},{13,4},{14,5},{15,6},{16,7},{17,8},{18,... | collective-permute-start | bytes 3080 | tf_op jit(solution)/shard_map/ppermute | solution.py:18
  959.0 31.0 %collective-permute-start.191 = (f32[256]{0:T(256)S(1)}, f32[256]{0:T(256)S(1)}, u32[]{:S(2)}, u32[]{:S(2)}) collective-permute-start(f32[256]{0:T(256)S(1)} %get-tuple-element.3), channel_id=1, source_target_pairs={{0,16},{1,17},{2,18},{3,19},{4,20},{5,21},{6,22},{7,23},{8,24},{9,... | collective-permute-start | bytes 3080 | tf_op jit(solution)/shard_map/ppermute | solution.py:18
  961.3 33.7 %collective-permute-start.161 = (f32[256]{0:T(256)S(1)}, f32[256]{0:T(256)S(1)}, u32[]{:S(2)}, u32[]{:S(2)}) collective-permute-start(f32[256]{0:T(256)S(1)} %get-tuple-element.21), channel_id=1, source_target_pairs={{15,0},{16,1},{17,2},{18,3},{19,4},{20,5},{21,6},{22,7},{23,8},{24... | collective-permute-start | bytes 3080 | tf_op jit(solution)/shard_map/ppermute | solution.py:18
  968.6 34.4 %collective-permute-start.162 = (f32[256]{0:T(256)S(1)}, f32[256]{0:T(256)S(1)}, u32[]{:S(2)}, u32[]{:S(2)}) collective-permute-start(f32[256]{0:T(256)S(1)} %get-tuple-element.33), channel_id=1, source_target_pairs={{14,0},{15,1},{16,2},{17,3},{18,4},{19,5},{20,6},{21,7},{22,8},{23... | collective-permute-start | bytes 3080 | tf_op jit(solution)/shard_map/ppermute | solution.py:18
  974.7 30.3 %collective-permute-start.163 = (f32[256]{0:T(256)S(1)}, f32[256]{0:T(256)S(1)}, u32[]{:S(2)}, u32[]{:S(2)}) collective-permute-start(f32[256]{0:T(256)S(1)} %get-tuple-element.32), channel_id=1, source_target_pairs={{13,0},{14,1},{15,2},{16,3},{17,4},{18,5},{19,6},{20,7},{21,8},{22... | collective-permute-start | bytes 3080 | tf_op jit(solution)/shard_map/ppermute | solution.py:18
  1099.8 31.8 %collective-permute-start.215 = (f32[256]{0:T(256)S(1)}, f32[256]{0:T(256)S(1)}, u32[]{:S(2)}, u32[]{:S(2)}) collective-permute-start(f32[256]{0:T(256)S(1)} %add_divide_fusion), channel_id=1, source_target_pairs={{8,0},{9,1},{10,2},{11,3},{12,4},{13,5},{14,6},{15,7},{16,8},{17,9... | collective-permute-start | bytes 3080 | tf_op jit(solution)/shard_map/ppermute | solution.py:18
  1104.3 31.2 %collective-permute-start.216 = (f32[256]{0:T(256)S(1)}, f32[256]{0:T(256)S(1)}, u32[]{:S(2)}, u32[]{:S(2)}) collective-permute-start(f32[256]{0:T(256)S(1)} %add_divide_fusion), channel_id=1, source_target_pairs={{9,0},{10,1},{11,2},{12,3},{13,4},{14,5},{15,6},{16,7},{17,8},{18,... | collective-permute-start | bytes 3080 | tf_op jit(solution)/shard_map/ppermute | solution.py:18
  (181 other events, 2848.4 us)
where the time goes:
time: 1200 us; the launch traced here: 1190 us
  starting transfers between devices  857 us (71%)
  waiting for transfers between devices  254 us (21%)
  other arithmetic  33.6 us (3%)
  matrix products  24.3 us (2%)
    ppermute x224, starting transfers between devices, shifted_2(): return lax.ppermute(block, axis, route)  844 us
    ppermute x224, waiting for transfers between devices, shifted_2(): return lax.ppermute(block, axis, route)  234 us
  transfers between devices with their start and end apart: 227, of which 42 were waited for; matrix products, arithmetic and copies ran while one was open for 1% of the time, Pallas kernels for 0%

commit v1 on v0

--- a/solution.py
+++ b/solution.py
@@ -74,25 +74,23 @@
     def kernel():
         return to_kernel(cosines())
 
+    padded_len = sentences + 2 * reach
+
+    def column_scaling(part):
+        full = lax.dynamic_update_slice_in_dim(
+            jnp.zeros((padded_len,), jnp.float32), part, first_row, 0
+        )
+        columns = lax.psum(full, ("seq", "emb"))
+        mine = lax.dynamic_slice_in_dim(columns, first_row, width, 0)
+        return jnp.where(valid, 1.0 / jnp.where(valid, mine, 1.0), 0.0)
+
     scaling = valid.astype(jnp.float32)
     inverse = jnp.zeros((rows_dev,), jnp.float32)
     for step in range(ITERS):
         kern = kernel()
         inverse = 1.0 / jnp.sum(kern * scaling[None, :], axis=1)
         part = jnp.sum(kern * inverse[:, None], axis=0)
-        owned = part[reach : reach + rows_dev]
-        for lag in range(-hops, hops + 1):
-            if lag != 0:
-                begin = reach + lag * rows_dev
-                owned = owned + shifted_2(part[begin : begin + rows_dev], ("seq", "emb"), lag)
-        own_scaling = 1.0 / owned
-        parts_list = []
-        for lag in range(-hops, hops + 1):
-            if lag == 0:
-                parts_list.append(own_scaling)
-            else:
-                parts_list.append(shifted_2(own_scaling, ("seq", "emb"), -lag))
-        scaling = jnp.concatenate(parts_list, axis=0)
+        scaling = column_scaling(part)
     kern = kernel()
     totals = jnp.sum(kern * scaling[None, :], axis=1)
     row_mass = inverse * totals

time: 1200 us -> 918 us (0.77)
  starting transfers between devices: 857 us -> 177 us
  waiting for transfers between devices: 254 us -> 650 us
    ppermute x224 -> x32, starting transfers between devices: 844 us -> 164 us  [shifted_2(): return lax.ppermute(block, axis, route)]
    psum x0 -> x3, waiting for transfers between devices: none -> 424 us  [column_scaling(): columns = lax.psum(full, ('seq', 'emb'))]
    ppermute x224 -> x32, waiting for transfers between devices: 234 us -> 205 us  [shifted_2(): return lax.ppermute(block, axis, route)]
  transfers between devices with their start and end apart: 227 -> 38, of which waited for: 42 -> 27; matrix products, arithmetic and copies ran while one was open for 1% -> 1% of each run, Pallas kernels for 0% -> 0%
where the time goes in v1:
time: 918 us; the launch traced here: 914 us
  waiting for transfers between devices  650 us (71%)
  starting transfers between devices  177 us (19%)
  other arithmetic  35.1 us (4%)
  matrix products  24.3 us (3%)
  between operations  14.5 us (2%)
  local copies, waits for them, and re-layouts  14 us (2%)
    psum x3, waiting for transfers between devices, column_scaling(): columns = lax.psum(full, ('seq', 'emb'))  424 us
    ppermute x32, waiting for transfers between devices, shifted_2(): return lax.ppermute(block, axis, route)  205 us
    ppermute x32, starting transfers between devices, shifted_2(): return lax.ppermute(block, axis, route)  164 us
  transfers between devices with their start and end apart: 38, of which 27 were waited for; matrix products, arithmetic and copies ran while one was open for 1% of the time, Pallas kernels for 0%

profile of v1, /device:TPU:26, one launch (start us, length us, event | category | flops | bytes accessed | tf_op | source)
XLA Modules:
  0.0 914.1 jit_solution(1106504656335570832)
XLA Ops:
  7.2 5.3 all-to-all-start
  12.5 10.3 %all-to-all-done = bf16[8,256,128]{2,1,0:T(8,128)(2,1)S(1)} async-done(((bf16[8,256,128]{2,1,0:T(8,128)(2,1)}), bf16[8,256,128]{2,1,0:T(8,128)(2,1)S(1)}, u32[]{:S(2)}, u32[]{:S(2)}) %all-to-all-start) | async-done | bytes 524320 | tf_op jit(solution)/shard_map/all_to_all | solution.py:31
  22.8 3.5 all-to-all-start.1
  27.4 4.0 collective-permute-start
  31.5 2.9 collective-permute-start.1
  42.2 4.4 collective-permute-done
  49.6 11.1 %collective-permute-done.1 = bf16[256,1024]{0,1:T(8,128)(2,1)S(1)} collective-permute-done((bf16[256,1024]{0,1:T(8,128)(2,1)S(1)}, bf16[256,1024]{0,1:T(8,128)(2,1)S(1)}, u32[]{:S(2)}, u32[]{:S(2)}) %collective-permute-start.1) | collective-permute-done | bytes 524320 | tf_op jit(solution)/shard_map/ppermute | solution.py:18
  62.7 10.9 %collective-permute-done.2 = bf16[256,1024]{0,1:T(8,128)(2,1)} collective-permute-done((bf16[256,1024]{0,1:T(8,128)(2,1)S(1)}, bf16[256,1024]{0,1:T(8,128)(2,1)}, u32[]{:S(2)}, u32[]{:S(2)}) %collective-permute-start.2) | collective-permute-done | bytes 524320 | tf_op jit(solution)/shard_map/ppermute | solution.py:18
  76.6 8.2 collective-permute-done.3
  86.8 9.3 %collective-permute-done.4 = bf16[256,1024]{0,1:T(8,128)(2,1)S(1)} collective-permute-done((bf16[256,1024]{0,1:T(8,128)(2,1)S(1)}, bf16[256,1024]{0,1:T(8,128)(2,1)S(1)}, u32[]{:S(2)}, u32[]{:S(2)}) %collective-permute-start.4) | collective-permute-done | bytes 524320 | tf_op jit(solution)/shard_map/ppermute | solution.py:18
  98.0 9.4 %collective-permute-done.5 = bf16[256,1024]{0,1:T(8,128)(2,1)S(1)} collective-permute-done((bf16[256,1024]{0,1:T(8,128)(2,1)S(1)}, bf16[256,1024]{0,1:T(8,128)(2,1)S(1)}, u32[]{:S(2)}, u32[]{:S(2)}) %collective-permute-start.5) | collective-permute-done | bytes 524320 | tf_op jit(solution)/shard_map/ppermute | solution.py:18
  109.4 9.3 %collective-permute-done.6 = bf16[256,1024]{0,1:T(8,128)(2,1)S(1)} collective-permute-done((bf16[256,1024]{0,1:T(8,128)(2,1)S(1)}, bf16[256,1024]{0,1:T(8,128)(2,1)S(1)}, u32[]{:S(2)}, u32[]{:S(2)}) %collective-permute-start.6) | collective-permute-done | bytes 524320 | tf_op jit(solution)/shard_map/ppermute | solution.py:18
  120.7 9.3 %collective-permute-done.7 = bf16[256,1024]{0,1:T(8,128)(2,1)S(1)} collective-permute-done((bf16[256,1024]{0,1:T(8,128)(2,1)S(1)}, bf16[256,1024]{0,1:T(8,128)(2,1)S(1)}, u32[]{:S(2)}, u32[]{:S(2)}) %collective-permute-start.7) | collective-permute-done | bytes 524320 | tf_op jit(solution)/shard_map/ppermute | solution.py:18
  129.9 3.3 collective-permute-start.12
  133.3 7.9 collective-permute-done.8
  143.1 12.5 %collective-permute-start.14 = (bf16[256,1024]{0,1:T(8,128)(2,1)S(1)}, bf16[256,1024]{0,1:T(8,128)(2,1)S(1)}, u32[]{:S(2)}, u32[]{:S(2)}) collective-permute-start(bf16[256,1024]{0,1:T(8,128)(2,1)S(1)} %bitcast.43), channel_id=1, source_target_pairs={{0,2},{1,3},{2,4},{3,5},{4,6},{5,7},{6,8},{7,9},{8,10},{9,11},{10,... | collective-permute-start | bytes 1572872 | tf_op jit(solution)/shard_map/ppermute | solution.py:18
  155.6 4.8 collective-permute-done.10
  162.4 2.8 collective-permute-done.11
  165.2 6.5 collective-permute-start.16
  171.8 13.0 %collective-permute-done.12 = bf16[256,1024]{0,1:T(8,128)(2,1)S(1)} collective-permute-done((bf16[256,1024]{0,1:T(8,128)(2,1)S(1)}, bf16[256,1024]{0,1:T(8,128)(2,1)S(1)}, u32[]{:S(2)}, u32[]{:S(2)}) %collective-permute-start.12) | collective-permute-done | bytes 524320 | tf_op jit(solution)/shard_map/ppermute | solution.py:18
  186.8 6.4 collective-permute-done.13
  195.2 16.5 %collective-permute-done.14 = bf16[256,1024]{0,1:T(8,128)(2,1)S(1)} collective-permute-done((bf16[256,1024]{0,1:T(8,128)(2,1)S(1)}, bf16[256,1024]{0,1:T(8,128)(2,1)S(1)}, u32[]{:S(2)}, u32[]{:S(2)}) %collective-permute-start.14) | collective-permute-done | bytes 524320 | tf_op jit(solution)/shard_map/ppermute | solution.py:18
  213.7 6.8 collective-permute-done.15
  226.5 5.7 collective-permute-start.23
  232.3 21.5 %collective-permute-done.19 = bf16[256,1024]{0,1:T(8,128)(2,1)S(1)} collective-permute-done((bf16[256,1024]{0,1:T(8,128)(2,1)S(1)}, bf16[256,1024]{0,1:T(8,128)(2,1)S(1)}, u32[]{:S(2)}, u32[]{:S(2)}) %collective-permute-start.19) | collective-permute-done | bytes 524320 | tf_op jit(solution)/shard_map/ppermute | solution.py:18
  258.7 4.1 collective-permute-start.26
  262.9 4.6 collective-permute-start.27
  267.5 6.5 collective-permute-done.23
  275.9 3.7 collective-permute-done.24
  279.7 17.7 %collective-permute-start.29 = (bf16[256,1024]{0,1:T(8,128)(2,1)S(1)}, bf16[256,1024]{0,1:T(8,128)(2,1)S(1)}, u32[]{:S(2)}, u32[]{:S(2)}) collective-permute-start(bf16[256,1024]{0,1:T(8,128)(2,1)S(1)} %bitcast.59), channel_id=1, source_target_pairs={{14,0},{15,1},{16,2},{17,3},{18,4},{19,5},{20,6},{21,7},{22,8},{23... | collective-permute-start | bytes 1572872 | tf_op jit(solution)/shard_map/ppermute | solution.py:18
  297.4 4.8 collective-permute-done.25
  304.2 2.8 collective-permute-done.26
  307.0 60.8 %collective-permute-start.31 = (bf16[256,1024]{0,1:T(8,128)(2,1)S(1)}, bf16[256,1024]{0,1:T(8,128)(2,1)S(1)}, u32[]{:S(2)}, u32[]{:S(2)}) collective-permute-start(bf16[256,1024]{0,1:T(8,128)(2,1)S(1)} %bitcast.61), channel_id=1, source_target_pairs={{16,0},{17,1},{18,2},{19,3},{20,4},{21,5},{22,6},{23,7},{24,8},{25... | collective-permute-start | bytes 1572872 | tf_op jit(solution)/shard_map/ppermute | solution.py:18
  368.1 34.7 %collective-permute-done.31 = bf16[256,1024]{0,1:T(8,128)(2,1)S(1)} collective-permute-done((bf16[256,1024]{0,1:T(8,128)(2,1)S(1)}, bf16[256,1024]{0,1:T(8,128)(2,1)S(1)}, u32[]{:S(2)}, u32[]{:S(2)}) %collective-permute-start.31) | collective-permute-done | bytes 524320 | tf_op jit(solution)/shard_map/ppermute | solution.py:18
  402.8 4.0 multiply_reduce_fusion
  406.8 11.5 %multiply_reduce_fusion.6 = (f32[256]{0:T(256)S(1)}, f32[256,8448]{0,1:T(8,128)S(1)}) fusion(f32[8448]{0:T(1024)S(1)} %get-tuple-element.5, s32[8448]{0:T(1024)S(1)} %get-tuple-element.6, s32[256]{0:T(256)S(1)} %dynamic_slice.15, f32[8448]{0:T(1024)S(1)} %add_rsqrt_fusion, f32[256]{0:T(256)S(1)} %add_rsqrt_fusion.1, ...), kind=kOutput, calls=%fused_computation.14 | convolution fusion | flops 4459462656 | bytes 26625280 | tf_op jit(solution)/shard_map/dot_general | solution.py:66
  418.3 3.4 copy-done
  424.3 140.6 %all-reduce.5.cloned.1.call-done = f32[40960]{0:T(1024)} async-done(((f32[40960]{0:T(1024)}), f32[40960]{0:T(1024)}) %all-reduce.5.cloned.1.call-update) | async-done | bytes 163856 | tf_op jit(solution)/shard_map/psum | solution.py:83
  565.8 5.7 multiply_reduce_fusion.4
  571.5 4.2 multiply_reduce_fusion.3
  577.1 141.8 %all-reduce.7.cloned.1.call-done = f32[40960]{0:T(1024)} async-done(((f32[40960]{0:T(1024)}), f32[40960]{0:T(1024)}) %all-reduce.7.cloned.1.call-update) | async-done | bytes 163856 | tf_op jit(solution)/shard_map/psum | solution.py:83
  719.7 5.7 multiply_reduce_fusion.2
  725.5 4.2 multiply_reduce_fusion.1
  730.9 141.8 %all-reduce.9.cloned.1.call-done = f32[40960]{0:T(1024)} async-done(((f32[40960]{0:T(1024)}), f32[40960]{0:T(1024)}) %all-reduce.9.cloned.1.call-update) | async-done | bytes 163856 | tf_op jit(solution)/shard_map/psum | solution.py:83
  873.6 5.7 multiply_reduce_fusion.7
  879.4 12.8 %fusion.11 = bf16[32,8,8,128]{3,2,1,0:T(8,128)(2,1)S(1)} fusion(bf16[8448,1024]{0,1:T(8,128)(2,1)} %copy-done.1, f32[256,8448]{0,1:T(8,128)} %copy-done, f32[256]{0:T(256)S(1)} %multiply_reduce_fusion.7, f32[8448]{0:T(1024)S(1)} %divide_select_fusion), kind=kOutput, calls=%fused_computation.22 | convolution fusion | flops 4435935232 | bytes 26511360 | tf_op jit(solution)/shard_map/dot_general | solution.py:98
  893.0 3.5 all-to-all-start.2
  897.1 9.7 %all-to-all-done.2 = bf16[256,8,128]{2,0,1:T(8,128)(2,1)S(1)} async-done(((bf16[256,8,128]{2,0,1:T(8,128)(2,1)}), bf16[256,8,128]{2,0,1:T(8,128)(2,1)S(1)}, u32[]{:S(2)}, u32[]{:S(2)}) %all-to-all-start.2) | async-done | bytes 524320 | tf_op jit(solution)/shard_map/all_to_all | solution.py:99
  (109 shorter events, 59.4 us)
Async XLA Ops:
  7.2 15.6 %all-to-all-start = ((bf16[8,256,128]{2,1,0:T(8,128)(2,1)}), bf16[8,256,128]{2,1,0:T(8,128)(2,1)S(1)}, u32[]{:S(2)}, u32[]{:S(2)}) async-start(bf16[8,256,128]{2,1,0:T(8,128)(2,1)} %bitcast.64), calls=%async_computation | async-start | bytes 1048576 | tf_op jit(solution)/shard_map/all_to_all | solution.py:31
  22.8 19.0 %all-to-all-start.1 = ((bf16[8,256,128]{2,1,0:T(8,128)(2,1)}), bf16[8,256,128]{2,1,0:T(8,128)(2,1)S(1)}, u32[]{:S(2)}, u32[]{:S(2)}) async-start(bf16[8,256,128]{2,1,0:T(8,128)(2,1)} %bitcast.65), calls=%async_computation.1 | async-start | bytes 1048576 | tf_op jit(solution)/shard_map/all_to_all | solution.py:30
  26.3 538.6 %all-reduce.5.cloned.1.call-start = ((), (), s32[]{:S(2)}) async-start(), calls=%async_computation.3 | async-start | bytes 327680 | tf_op jit(solution)/shard_map/psum | solution.py:83
  27.4 19.2 %collective-permute-start = (bf16[256,1024]{0,1:T(8,128)(2,1)S(1)}, bf16[256,1024]{0,1:T(8,128)(2,1)}, u32[]{:S(2)}, u32[]{:S(2)}) collective-permute-start(bf16[256,1024]{0,1:T(8,128)(2,1)S(1)} %bitcast.29), channel_id=1, source_target_pairs={{0,16},{1,17},{2,18},{3,19},{4,20},{5,21},{6,22},{7,23},{8,24},{9,... | collective-permute-start | bytes 1572872 | tf_op jit(solution)/shard_map/ppermute | solution.py:18
  31.5 29.3 %collective-permute-start.1 = (bf16[256,1024]{0,1:T(8,128)(2,1)S(1)}, bf16[256,1024]{0,1:T(8,128)(2,1)S(1)}, u32[]{:S(2)}, u32[]{:S(2)}) collective-permute-start(bf16[256,1024]{0,1:T(8,128)(2,1)S(1)} %bitcast.30), channel_id=1, source_target_pairs={{0,15},{1,16},{2,17},{3,18},{4,19},{5,20},{6,21},{7,22},{8,23},{9,... | collective-permute-start | bytes 1572872 | tf_op jit(solution)/shard_map/ppermute | solution.py:18
  36.0 37.6 %collective-permute-start.2 = (bf16[256,1024]{0,1:T(8,128)(2,1)S(1)}, bf16[256,1024]{0,1:T(8,128)(2,1)}, u32[]{:S(2)}, u32[]{:S(2)}) collective-permute-start(bf16[256,1024]{0,1:T(8,128)(2,1)S(1)} %bitcast.31), channel_id=1, source_target_pairs={{0,14},{1,15},{2,16},{3,17},{4,18},{5,19},{6,20},{7,21},{8,22},{9,... | collective-permute-start | bytes 1572872 | tf_op jit(solution)/shard_map/ppermute | solution.py:18
  37.9 46.9 %collective-permute-start.3 = (bf16[256,1024]{0,1:T(8,128)(2,1)S(1)}, bf16[256,1024]{0,1:T(8,128)(2,1)S(1)}, u32[]{:S(2)}, u32[]{:S(2)}) collective-permute-start(bf16[256,1024]{0,1:T(8,128)(2,1)S(1)} %bitcast.32), channel_id=1, source_target_pairs={{0,13},{1,14},{2,15},{3,16},{4,17},{5,18},{6,19},{7,20},{8,21},{9,... | collective-permute-start | bytes 1572872 | tf_op jit(solution)/shard_map/ppermute | solution.py:18
  39.9 56.2 %collective-permute-start.4 = (bf16[256,1024]{0,1:T(8,128)(2,1)S(1)}, bf16[256,1024]{0,1:T(8,128)(2,1)S(1)}, u32[]{:S(2)}, u32[]{:S(2)}) collective-permute-start(bf16[256,1024]{0,1:T(8,128)(2,1)S(1)} %bitcast.33), channel_id=1, source_target_pairs={{0,12},{1,13},{2,14},{3,15},{4,16},{5,17},{6,18},{7,19},{8,20},{9,... | collective-permute-start | bytes 1572872 | tf_op jit(solution)/shard_map/ppermute | solution.py:18
  46.6 60.8 %collective-permute-start.5 = (bf16[256,1024]{0,1:T(8,128)(2,1)S(1)}, bf16[256,1024]{0,1:T(8,128)(2,1)S(1)}, u32[]{:S(2)}, u32[]{:S(2)}) collective-permute-start(bf16[256,1024]{0,1:T(8,128)(2,1)S(1)} %bitcast.34), channel_id=1, source_target_pairs={{0,11},{1,12},{2,13},{3,14},{4,15},{5,16},{6,17},{7,18},{8,19},{9,... | collective-permute-start | bytes 1572872 | tf_op jit(solution)/shard_map/ppermute | solution.py:18
  60.8 57.9 %collective-permute-start.6 = (bf16[256,1024]{0,1:T(8,128)(2,1)S(1)}, bf16[256,1024]{0,1:T(8,128)(2,1)S(1)}, u32[]{:S(2)}, u32[]{:S(2)}) collective-permute-start(bf16[256,1024]{0,1:T(8,128)(2,1)S(1)} %bitcast.35), channel_id=1, source_target_pairs={{0,10},{1,11},{2,12},{3,13},{4,14},{5,15},{6,16},{7,17},{8,18},{9,... | collective-permute-start | bytes 1572872 | tf_op jit(solution)/shard_map/ppermute | solution.py:18
  73.6 56.3 %collective-permute-start.7 = (bf16[256,1024]{0,1:T(8,128)(2,1)S(1)}, bf16[256,1024]{0,1:T(8,128)(2,1)S(1)}, u32[]{:S(2)}, u32[]{:S(2)}) collective-permute-start(bf16[256,1024]{0,1:T(8,128)(2,1)S(1)} %bitcast.36), channel_id=1, source_target_pairs={{0,9},{1,10},{2,11},{3,12},{4,13},{5,14},{6,15},{7,16},{8,17},{9,1... | collective-permute-start | bytes 1572872 | tf_op jit(solution)/shard_map/ppermute | solution.py:18
  84.8 56.3 %collective-permute-start.8 = (bf16[256,1024]{0,1:T(8,128)(2,1)S(1)}, bf16[256,1024]{0,1:T(8,128)(2,1)S(1)}, u32[]{:S(2)}, u32[]{:S(2)}) collective-permute-start(bf16[256,1024]{0,1:T(8,128)(2,1)S(1)} %bitcast.37), channel_id=1, source_target_pairs={{0,8},{1,9},{2,10},{3,11},{4,12},{5,13},{6,14},{7,15},{8,16},{9,17... | collective-permute-start | bytes 1572872 | tf_op jit(solution)/shard_map/ppermute | solution.py:18
  96.1 47.1 %collective-permute-start.9 = (bf16[256,1024]{0,1:T(8,128)(2,1)S(1)}, bf16[256,1024]{0,1:T(8,128)(2,1)S(1)}, u32[]{:S(2)}, u32[]{:S(2)}) collective-permute-start(bf16[256,1024]{0,1:T(8,128)(2,1)S(1)} %bitcast.38), channel_id=1, source_target_pairs={{0,7},{1,8},{2,9},{3,10},{4,11},{5,12},{6,13},{7,14},{8,15},{9,16}... | collective-permute-start | bytes 1572872 | tf_op jit(solution)/shard_map/ppermute | solution.py:18
  107.5 53.0 %collective-permute-start.10 = (bf16[256,1024]{0,1:T(8,128)(2,1)S(1)}, bf16[256,1024]{0,1:T(8,128)(2,1)S(1)}, u32[]{:S(2)}, u32[]{:S(2)}) collective-permute-start(bf16[256,1024]{0,1:T(8,128)(2,1)S(1)} %bitcast.39), channel_id=1, source_target_pairs={{0,6},{1,7},{2,8},{3,9},{4,10},{5,11},{6,12},{7,13},{8,14},{9,15},... | collective-permute-start | bytes 1572872 | tf_op jit(solution)/shard_map/ppermute | solution.py:18
  118.7 46.5 %collective-permute-start.11 = (bf16[256,1024]{0,1:T(8,128)(2,1)S(1)}, bf16[256,1024]{0,1:T(8,128)(2,1)S(1)}, u32[]{:S(2)}, u32[]{:S(2)}) collective-permute-start(bf16[256,1024]{0,1:T(8,128)(2,1)S(1)} %bitcast.40), channel_id=1, source_target_pairs={{0,5},{1,6},{2,7},{3,8},{4,9},{5,10},{6,11},{7,12},{8,13},{9,14},{... | collective-permute-start | bytes 1572872 | tf_op jit(solution)/shard_map/ppermute | solution.py:18
  129.9 54.9 %collective-permute-start.12 = (bf16[256,1024]{0,1:T(8,128)(2,1)S(1)}, bf16[256,1024]{0,1:T(8,128)(2,1)S(1)}, u32[]{:S(2)}, u32[]{:S(2)}) collective-permute-start(bf16[256,1024]{0,1:T(8,128)(2,1)S(1)} %bitcast.41), channel_id=1, source_target_pairs={{0,4},{1,5},{2,6},{3,7},{4,8},{5,9},{6,10},{7,11},{8,12},{9,13},{1... | collective-permute-start | bytes 1572872 | tf_op jit(solution)/shard_map/ppermute | solution.py:18
  141.2 52.1 %collective-permute-start.13 = (bf16[256,1024]{0,1:T(8,128)(2,1)S(1)}, bf16[256,1024]{0,1:T(8,128)(2,1)S(1)}, u32[]{:S(2)}, u32[]{:S(2)}) collective-permute-start(bf16[256,1024]{0,1:T(8,128)(2,1)S(1)} %bitcast.42), channel_id=1, source_target_pairs={{0,3},{1,4},{2,5},{3,6},{4,7},{5,8},{6,9},{7,10},{8,11},{9,12},{10... | collective-permute-start | bytes 1572872 | tf_op jit(solution)/shard_map/ppermute | solution.py:18
  143.1 68.6 %collective-permute-start.14 = (bf16[256,1024]{0,1:T(8,128)(2,1)S(1)}, bf16[256,1024]{0,1:T(8,128)(2,1)S(1)}, u32[]{:S(2)}, u32[]{:S(2)}) collective-permute-start(bf16[256,1024]{0,1:T(8,128)(2,1)S(1)} %bitcast.43), channel_id=1, source_target_pairs={{0,2},{1,3},{2,4},{3,5},{4,6},{5,7},{6,8},{7,9},{8,10},{9,11},{10,... | collective-permute-start | bytes 1572872 | tf_op jit(solution)/shard_map/ppermute | solution.py:18
  160.5 60.1 %collective-permute-start.15 = (bf16[256,1024]{0,1:T(8,128)(2,1)S(1)}, bf16[256,1024]{0,1:T(8,128)(2,1)S(1)}, u32[]{:S(2)}, u32[]{:S(2)}) collective-permute-start(bf16[256,1024]{0,1:T(8,128)(2,1)S(1)} %bitcast.44), channel_id=1, source_target_pairs={{0,1},{1,2},{2,3},{3,4},{4,5},{5,6},{6,7},{7,8},{8,9},{9,10},{10,1... | collective-permute-start | bytes 1572872 | tf_op jit(solution)/shard_map/ppermute | solution.py:18
  165.2 57.3 %collective-permute-start.16 = (bf16[256,1024]{0,1:T(8,128)(2,1)S(1)}, bf16[256,1024]{0,1:T(8,128)(2,1)S(1)}, u32[]{:S(2)}, u32[]{:S(2)}) collective-permute-start(bf16[256,1024]{0,1:T(8,128)(2,1)S(1)} %bitcast.45), channel_id=1, source_target_pairs={{1,0},{2,1},{3,2},{4,3},{5,4},{6,5},{7,6},{8,7},{9,8},{10,9},{11,1... | collective-permute-start | bytes 1572872 | tf_op jit(solution)/shard_map/ppermute | solution.py:18
  184.9 39.7 %collective-permute-start.17 = (bf16[256,1024]{0,1:T(8,128)(2,1)S(1)}, bf16[256,1024]{0,1:T(8,128)(2,1)S(1)}, u32[]{:S(2)}, u32[]{:S(2)}) collective-permute-start(bf16[256,1024]{0,1:T(8,128)(2,1)S(1)} %bitcast.46), channel_id=1, source_target_pairs={{2,0},{3,1},{4,2},{5,3},{6,4},{7,5},{8,6},{9,7},{10,8},{11,9},{12,... | collective-permute-start | bytes 1572872 | tf_op jit(solution)/shard_map/ppermute | solution.py:18
  193.2 33.3 %collective-permute-start.18 = (bf16[256,1024]{0,1:T(8,128)(2,1)S(1)}, bf16[256,1024]{0,1:T(8,128)(2,1)S(1)}, u32[]{:S(2)}, u32[]{:S(2)}) collective-permute-start(bf16[256,1024]{0,1:T(8,128)(2,1)S(1)} %bitcast.47), channel_id=1, source_target_pairs={{3,0},{4,1},{5,2},{6,3},{7,4},{8,5},{9,6},{10,7},{11,8},{12,9},{13... | collective-permute-start | bytes 1572872 | tf_op jit(solution)/shard_map/ppermute | solution.py:18
  211.7 42.1 %collective-permute-start.19 = (bf16[256,1024]{0,1:T(8,128)(2,1)S(1)}, bf16[256,1024]{0,1:T(8,128)(2,1)S(1)}, u32[]{:S(2)}, u32[]{:S(2)}) collective-permute-start(bf16[256,1024]{0,1:T(8,128)(2,1)S(1)} %bitcast.48), channel_id=1, source_target_pairs={{4,0},{5,1},{6,2},{7,3},{8,4},{9,5},{10,6},{11,7},{12,8},{13,9},{1... | collective-permute-start | bytes 1572872 | tf_op jit(solution)/shard_map/ppermute | solution.py:18
  220.5 36.2 %collective-permute-start.20 = (bf16[256,1024]{0,1:T(8,128)(2,1)S(1)}, bf16[256,1024]{0,1:T(8,128)(2,1)S(1)}, u32[]{:S(2)}, u32[]{:S(2)}) collective-permute-start(bf16[256,1024]{0,1:T(8,128)(2,1)S(1)} %bitcast.49), channel_id=1, source_target_pairs={{5,0},{6,1},{7,2},{8,3},{9,4},{10,5},{11,6},{12,7},{13,8},{14,9},{... | collective-permute-start | bytes 1572872 | tf_op jit(solution)/shard_map/ppermute | solution.py:18
  222.5 36.2 %collective-permute-start.21 = (bf16[256,1024]{0,1:T(8,128)(2,1)S(1)}, bf16[256,1024]{0,1:T(8,128)(2,1)S(1)}, u32[]{:S(2)}, u32[]{:S(2)}) collective-permute-start(bf16[256,1024]{0,1:T(8,128)(2,1)S(1)} %bitcast.51), channel_id=1, source_target_pairs={{6,0},{7,1},{8,2},{9,3},{10,4},{11,5},{12,6},{13,7},{14,8},{15,9},... | collective-permute-start | bytes 1572872 | tf_op jit(solution)/shard_map/ppermute | solution.py:18
  224.5 38.3 %collective-permute-start.22 = (bf16[256,1024]{0,1:T(8,128)(2,1)S(1)}, bf16[256,1024]{0,1:T(8,128)(2,1)S(1)}, u32[]{:S(2)}, u32[]{:S(2)}) collective-permute-start(bf16[256,1024]{0,1:T(8,128)(2,1)S(1)} %bitcast.52), channel_id=1, source_target_pairs={{7,0},{8,1},{9,2},{10,3},{11,4},{12,5},{13,6},{14,7},{15,8},{16,9}... | collective-permute-start | bytes 1572872 | tf_op jit(solution)/shard_map/ppermute | solution.py:18
  226.5 47.5 %collective-permute-start.23 = (bf16[256,1024]{0,1:T(8,128)(2,1)S(1)}, bf16[256,1024]{0,1:T(8,128)(2,1)S(1)}, u32[]{:S(2)}, u32[]{:S(2)}) collective-permute-start(bf16[256,1024]{0,1:T(8,128)(2,1)S(1)} %bitcast.53), channel_id=1, source_target_pairs={{8,0},{9,1},{10,2},{11,3},{12,4},{13,5},{14,6},{15,7},{16,8},{17,9... | collective-permute-start | bytes 1572872 | tf_op jit(solution)/shard_map/ppermute | solution.py:18
  253.8 25.8 %collective-permute-start.24 = (bf16[256,1024]{0,1:T(8,128)(2,1)S(1)}, bf16[256,1024]{0,1:T(8,128)(2,1)S(1)}, u32[]{:S(2)}, u32[]{:S(2)}) collective-permute-start(bf16[256,1024]{0,1:T(8,128)(2,1)S(1)} %bitcast.54), channel_id=1, source_target_pairs={{9,0},{10,1},{11,2},{12,3},{13,4},{14,5},{15,6},{16,7},{17,8},{18,... | collective-permute-start | bytes 1572872 | tf_op jit(solution)/shard_map/ppermute | solution.py:18
  256.8 45.4 %collective-permute-start.25 = (bf16[256,1024]{0,1:T(8,128)(2,1)S(1)}, bf16[256,1024]{0,1:T(8,128)(2,1)S(1)}, u32[]{:S(2)}, u32[]{:S(2)}) collective-permute-start(bf16[256,1024]{0,1:T(8,128)(2,1)S(1)} %bitcast.55), channel_id=1, source_target_pairs={{10,0},{11,1},{12,2},{13,3},{14,4},{15,5},{16,6},{17,7},{18,8},{19... | collective-permute-start | bytes 1572872 | tf_op jit(solution)/shard_map/ppermute | solution.py:18
  258.7 48.3 %collective-permute-start.26 = (bf16[256,1024]{0,1:T(8,128)(2,1)S(1)}, bf16[256,1024]{0,1:T(8,128)(2,1)S(1)}, u32[]{:S(2)}, u32[]{:S(2)}) collective-permute-start(bf16[256,1024]{0,1:T(8,128)(2,1)S(1)} %bitcast.56), channel_id=1, source_target_pairs={{11,0},{12,1},{13,2},{14,3},{15,4},{16,5},{17,6},{18,7},{19,8},{20... | collective-permute-start | bytes 1572872 | tf_op jit(solution)/shard_map/ppermute | solution.py:18
  262.9 105.0 %collective-permute-start.27 = (bf16[256,1024]{0,1:T(8,128)(2,1)S(1)}, bf16[256,1024]{0,1:T(8,128)(2,1)S(1)}, u32[]{:S(2)}, u32[]{:S(2)}) collective-permute-start(bf16[256,1024]{0,1:T(8,128)(2,1)S(1)} %bitcast.57), channel_id=1, source_target_pairs={{12,0},{13,1},{14,2},{15,3},{16,4},{17,5},{18,6},{19,7},{20,8},{21... | collective-permute-start | bytes 1572872 | tf_op jit(solution)/shard_map/ppermute | solution.py:18
  274.0 93.9 %collective-permute-start.28 = (bf16[256,1024]{0,1:T(8,128)(2,1)S(1)}, bf16[256,1024]{0,1:T(8,128)(2,1)S(1)}, u32[]{:S(2)}, u32[]{:S(2)}) collective-permute-start(bf16[256,1024]{0,1:T(8,128)(2,1)S(1)} %bitcast.58), channel_id=1, source_target_pairs={{13,0},{14,1},{15,2},{16,3},{17,4},{18,5},{19,6},{20,7},{21,8},{22... | collective-permute-start | bytes 1572872 | tf_op jit(solution)/shard_map/ppermute | solution.py:18
  279.7 88.3 %collective-permute-start.29 = (bf16[256,1024]{0,1:T(8,128)(2,1)S(1)}, bf16[256,1024]{0,1:T(8,128)(2,1)S(1)}, u32[]{:S(2)}, u32[]{:S(2)}) collective-permute-start(bf16[256,1024]{0,1:T(8,128)(2,1)S(1)} %bitcast.59), channel_id=1, source_target_pairs={{14,0},{15,1},{16,2},{17,3},{18,4},{19,5},{20,6},{21,7},{22,8},{23... | collective-permute-start | bytes 1572872 | tf_op jit(solution)/shard_map/ppermute | solution.py:18
  302.2 65.8 %collective-permute-start.30 = (bf16[256,1024]{0,1:T(8,128)(2,1)S(1)}, bf16[256,1024]{0,1:T(8,128)(2,1)S(1)}, u32[]{:S(2)}, u32[]{:S(2)}) collective-permute-start(bf16[256,1024]{0,1:T(8,128)(2,1)S(1)} %bitcast.60), channel_id=1, source_target_pairs={{15,0},{16,1},{17,2},{18,3},{19,4},{20,5},{21,6},{22,7},{23,8},{24... | collective-permute-start | bytes 1572872 | tf_op jit(solution)/shard_map/ppermute | solution.py:18
  307.0 95.8 %collective-permute-start.31 = (bf16[256,1024]{0,1:T(8,128)(2,1)S(1)}, bf16[256,1024]{0,1:T(8,128)(2,1)S(1)}, u32[]{:S(2)}, u32[]{:S(2)}) collective-permute-start(bf16[256,1024]{0,1:T(8,128)(2,1)S(1)} %bitcast.61), channel_id=1, source_target_pairs={{16,0},{17,1},{18,2},{19,3},{20,4},{21,5},{22,6},{23,7},{24,8},{25... | collective-permute-start | bytes 1572872 | tf_op jit(solution)/shard_map/ppermute | solution.py:18
  402.8 15.5 %copy-start.1 = (bf16[8448,1024]{0,1:T(8,128)(2,1)}, bf16[8448,1024]{0,1:T(8,128)(2,1)S(1)}, u32[]{:S(2)}) copy-start(bf16[8448,1024]{0,1:T(8,128)(2,1)S(1)} %constant_dynamic-update-slice_fusion) | copy-start | bytes 51904516
  418.3 3.4 copy-start
  423.6 0.7 copy-start.3
  424.3 294.6 %all-reduce.7.cloned.1.call-start = ((), (), s32[]{:S(2)}) async-start(), calls=%async_computation.4 | async-start | bytes 327680 | tf_op jit(solution)/shard_map/psum | solution.py:83
  576.3 0.7 copy-start.4
  577.0 295.8 %all-reduce.9.cloned.1.call-start = ((), (), s32[]{:S(2)}) async-start(), calls=%async_computation.5 | async-start | bytes 327680 | tf_op jit(solution)/shard_map/psum | solution.py:83
  730.2 0.7 copy-start.2
  893.0 13.7 %all-to-all-start.2 = ((bf16[256,8,128]{2,0,1:T(8,128)(2,1)}), bf16[256,8,128]{2,0,1:T(8,128)(2,1)S(1)}, u32[]{:S(2)}, u32[]{:S(2)}) async-start(bf16[256,8,128]{2,0,1:T(8,128)(2,1)} %bitcast.27), calls=%async_computation.2 | async-start | bytes 1048576 | tf_op jit(solution)/shard_map/all_to_all | solution.py:99
Sparse Core Ops, SparseCore 0:
  424.4 140.5 all-reduce.4
  577.1 141.6 all-reduce.6
  731.1 141.6 all-reduce.8

commit v2 on v1

--- a/solution.py
+++ b/solution.py
@@ -74,14 +74,32 @@
     def kernel():
         return to_kernel(cosines())
 
-    padded_len = sentences + 2 * reach
+    n_emb_axis = lax.axis_size("emb")
+    block_rows = rows_dev * n_emb_axis
+    span = block_rows + 2 * reach
+    emb_index = lax.axis_index("emb")
+    seq_hops = reach // block_rows
+
+    def emb_sum(x):
+        step = 1
+        while step < n_emb_axis:
+            route = [(e, e ^ step) for e in range(n_emb_axis)]
+            x = x + lax.ppermute(x, "emb", route)
+            step *= 2
+        return x
 
     def column_scaling(part):
-        full = lax.dynamic_update_slice_in_dim(
-            jnp.zeros((padded_len,), jnp.float32), part, first_row, 0
+        block = lax.dynamic_update_slice_in_dim(
+            jnp.zeros((span,), jnp.float32), part, emb_index * rows_dev, 0
         )
-        columns = lax.psum(full, ("seq", "emb"))
-        mine = lax.dynamic_slice_in_dim(columns, first_row, width, 0)
+        block = emb_sum(block)
+        total = block
+        for d in range(1, 2 * seq_hops + 1):
+            keep = span - d * block_rows
+            upper = shifted_2(block[:keep], "seq", -d)
+            lower = shifted_2(block[d * block_rows :], "seq", d)
+            total = total + jnp.pad(upper, (d * block_rows, 0)) + jnp.pad(lower, (0, d * block_rows))
+        mine = lax.dynamic_slice_in_dim(total, emb_index * rows_dev, width, 0)
         return jnp.where(valid, 1.0 / jnp.where(valid, mine, 1.0), 0.0)
 
     scaling = valid.astype(jnp.float32)

time: 918 us -> 588 us (0.64)
  waiting for transfers between devices: 650 us -> 285 us
  starting transfers between devices: 177 us -> 220 us
  between operations: 14.5 us -> 2.3 us
    psum x3 -> x0, waiting for transfers between devices: 424 us -> none  [column_scaling(): columns = lax.psum(full, ('seq', 'emb'))]
    ppermute x32 -> x56, waiting for transfers between devices: 205 us -> 240 us  [shifted_2(): return lax.ppermute(block, axis, route)]
    ppermute x32 -> x56, starting transfers between devices: 164 us -> 194 us  [shifted_2(): return lax.ppermute(block, axis, route)]
    ppermute x0 -> x9, waiting for transfers between devices: none -> 25 us  [emb_sum(): x = x + lax.ppermute(x, 'emb', route)]
    ppermute x0 -> x9, starting transfers between devices: none -> 13.2 us  [emb_sum(): x = x + lax.ppermute(x, 'emb', route)]
  transfers between devices with their start and end apart: 38 -> 68, of which waited for: 27 -> 38; matrix products, arithmetic and copies ran while one was open for 1% -> 1% of each run, Pallas kernels for 0% -> 0%
where the time goes in v2:
time: 588 us; the launch traced here: 578 us
  waiting for transfers between devices  285 us (48%)
  starting transfers between devices  220 us (37%)
  other arithmetic  34.2 us (6%)
  matrix products  24.3 us (4%)
  local copies, waits for them, and re-layouts  12 us (2%)
    ppermute x56, waiting for transfers between devices, shifted_2(): return lax.ppermute(block, axis, route)  240 us
    ppermute x56, starting transfers between devices, shifted_2(): return lax.ppermute(block, axis, route)  194 us
    ppermute x9, waiting for transfers between devices, emb_sum(): x = x + lax.ppermute(x, 'emb', route)  25 us
    ppermute x9, starting transfers between devices, emb_sum(): x = x + lax.ppermute(x, 'emb', route)  13.2 us
    dot_general x1, matrix products, per_device(): jnp.dot(weights, window, preferred_element_type=jnp.float32)  12.8 us
  transfers between devices with their start and end apart: 68, of which 38 were waited for; matrix products, arithmetic and copies ran while one was open for 1% of the time, Pallas kernels for 0%

profile of v2, /device:TPU:26, one launch (start us, length us, event | category | flops | bytes accessed | tf_op | source)
XLA Modules:
  0.0 577.8 jit_solution(11150172839337129261)
XLA Ops:
  0.6 5.3 all-to-all-start
  6.0 10.3 %all-to-all-done = bf16[8,256,128]{2,1,0:T(8,128)(2,1)S(1)} async-done(((bf16[8,256,128]{2,1,0:T(8,128)(2,1)}), bf16[8,256,128]{2,1,0:T(8,128)(2,1)S(1)}, u32[]{:S(2)}, u32[]{:S(2)}) %all-to-all-start) | async-done | bytes 524320 | tf_op jit(solution)/shard_map/all_to_all | solution.py:31
  35.7 4.3 collective-permute-done
  41.9 12.3 %collective-permute-done.1 = bf16[256,1024]{0,1:T(8,128)(2,1)S(1)} collective-permute-done((bf16[256,1024]{0,1:T(8,128)(2,1)S(1)}, bf16[256,1024]{0,1:T(8,128)(2,1)S(1)}, u32[]{:S(2)}, u32[]{:S(2)}) %collective-permute-start.1) | collective-permute-done | bytes 524320 | tf_op jit(solution)/shard_map/ppermute | solution.py:18
  56.2 10.9 %collective-permute-done.2 = bf16[256,1024]{0,1:T(8,128)(2,1)} collective-permute-done((bf16[256,1024]{0,1:T(8,128)(2,1)S(1)}, bf16[256,1024]{0,1:T(8,128)(2,1)}, u32[]{:S(2)}, u32[]{:S(2)}) %collective-permute-start.2) | collective-permute-done | bytes 524320 | tf_op jit(solution)/shard_map/ppermute | solution.py:18
  70.1 8.2 %collective-permute-done.3 = bf16[256,1024]{0,1:T(8,128)(2,1)} collective-permute-done((bf16[256,1024]{0,1:T(8,128)(2,1)S(1)}, bf16[256,1024]{0,1:T(8,128)(2,1)}, u32[]{:S(2)}, u32[]{:S(2)}) %collective-permute-start.3) | collective-permute-done | bytes 524320 | tf_op jit(solution)/shard_map/ppermute | solution.py:18
  81.3 8.2 %collective-permute-done.4 = bf16[256,1024]{0,1:T(8,128)(2,1)S(1)} collective-permute-done((bf16[256,1024]{0,1:T(8,128)(2,1)S(1)}, bf16[256,1024]{0,1:T(8,128)(2,1)S(1)}, u32[]{:S(2)}, u32[]{:S(2)}) %collective-permute-start.4) | collective-permute-done | bytes 524320 | tf_op jit(solution)/shard_map/ppermute | solution.py:18
  91.5 9.4 %collective-permute-done.5 = bf16[256,1024]{0,1:T(8,128)(2,1)S(1)} collective-permute-done((bf16[256,1024]{0,1:T(8,128)(2,1)S(1)}, bf16[256,1024]{0,1:T(8,128)(2,1)S(1)}, u32[]{:S(2)}, u32[]{:S(2)}) %collective-permute-start.5) | collective-permute-done | bytes 524320 | tf_op jit(solution)/shard_map/ppermute | solution.py:18
  102.9 9.3 %collective-permute-done.6 = bf16[256,1024]{0,1:T(8,128)(2,1)S(1)} collective-permute-done((bf16[256,1024]{0,1:T(8,128)(2,1)S(1)}, bf16[256,1024]{0,1:T(8,128)(2,1)S(1)}, u32[]{:S(2)}, u32[]{:S(2)}) %collective-permute-start.6) | collective-permute-done | bytes 524320 | tf_op jit(solution)/shard_map/ppermute | solution.py:18
  114.1 9.3 %collective-permute-done.7 = bf16[256,1024]{0,1:T(8,128)(2,1)S(1)} collective-permute-done((bf16[256,1024]{0,1:T(8,128)(2,1)S(1)}, bf16[256,1024]{0,1:T(8,128)(2,1)S(1)}, u32[]{:S(2)}, u32[]{:S(2)}) %collective-permute-start.7) | collective-permute-done | bytes 524320 | tf_op jit(solution)/shard_map/ppermute | solution.py:18
  126.7 7.9 %collective-permute-done.8 = bf16[256,1024]{0,1:T(8,128)(2,1)S(1)} collective-permute-done((bf16[256,1024]{0,1:T(8,128)(2,1)S(1)}, bf16[256,1024]{0,1:T(8,128)(2,1)S(1)}, u32[]{:S(2)}, u32[]{:S(2)}) %collective-permute-start.8) | collective-permute-done | bytes 524320 | tf_op jit(solution)/shard_map/ppermute | solution.py:18
  136.6 18.7 %collective-permute-start.14 = (bf16[256,1024]{0,1:T(8,128)(2,1)S(1)}, bf16[256,1024]{0,1:T(8,128)(2,1)S(1)}, u32[]{:S(2)}, u32[]{:S(2)}) collective-permute-start(bf16[256,1024]{0,1:T(8,128)(2,1)S(1)} %bitcast.43), channel_id=1, source_target_pairs={{0,2},{1,3},{2,4},{3,5},{4,6},{5,7},{6,8},{7,9},{8,10},{9,11},{10,... | collective-permute-start | bytes 1572872 | tf_op jit(solution)/shard_map/ppermute | solution.py:18
  155.3 11.5 %collective-permute-start.15 = (bf16[256,1024]{0,1:T(8,128)(2,1)S(1)}, bf16[256,1024]{0,1:T(8,128)(2,1)S(1)}, u32[]{:S(2)}, u32[]{:S(2)}) collective-permute-start(bf16[256,1024]{0,1:T(8,128)(2,1)S(1)} %bitcast.44), channel_id=1, source_target_pairs={{0,1},{1,2},{2,3},{3,4},{4,5},{5,6},{6,7},{7,8},{8,9},{9,10},{10,1... | collective-permute-start | bytes 1572872 | tf_op jit(solution)/shard_map/ppermute | solution.py:18
  166.8 10.2 %collective-permute-start.16 = (bf16[256,1024]{0,1:T(8,128)(2,1)S(1)}, bf16[256,1024]{0,1:T(8,128)(2,1)S(1)}, u32[]{:S(2)}, u32[]{:S(2)}) collective-permute-start(bf16[256,1024]{0,1:T(8,128)(2,1)S(1)} %bitcast.45), channel_id=1, source_target_pairs={{1,0},{2,1},{3,2},{4,3},{5,4},{6,5},{7,6},{8,7},{9,8},{10,9},{11,1... | collective-permute-start | bytes 1572872 | tf_op jit(solution)/shard_map/ppermute | solution.py:18
  178.3 10.6 %collective-permute-start.17 = (bf16[256,1024]{0,1:T(8,128)(2,1)S(1)}, bf16[256,1024]{0,1:T(8,128)(2,1)S(1)}, u32[]{:S(2)}, u32[]{:S(2)}) collective-permute-start(bf16[256,1024]{0,1:T(8,128)(2,1)S(1)} %bitcast.46), channel_id=1, source_target_pairs={{2,0},{3,1},{4,2},{5,3},{6,4},{7,5},{8,6},{9,7},{10,8},{11,9},{12,... | collective-permute-start | bytes 1572872 | tf_op jit(solution)/shard_map/ppermute | solution.py:18
  189.0 5.1 collective-permute-start.18
  194.2 9.9 %collective-permute-done.14 = bf16[256,1024]{0,1:T(8,128)(2,1)S(1)} collective-permute-done((bf16[256,1024]{0,1:T(8,128)(2,1)S(1)}, bf16[256,1024]{0,1:T(8,128)(2,1)S(1)}, u32[]{:S(2)}, u32[]{:S(2)}) %collective-permute-start.14) | collective-permute-done | bytes 524320 | tf_op jit(solution)/shard_map/ppermute | solution.py:18
  206.1 7.7 %collective-permute-done.15 = bf16[256,1024]{0,1:T(8,128)(2,1)S(1)} collective-permute-done((bf16[256,1024]{0,1:T(8,128)(2,1)S(1)}, bf16[256,1024]{0,1:T(8,128)(2,1)S(1)}, u32[]{:S(2)}, u32[]{:S(2)}) %collective-permute-start.15) | collective-permute-done | bytes 524320 | tf_op jit(solution)/shard_map/ppermute | solution.py:18
  219.7 9.7 %collective-permute-done.18 = bf16[256,1024]{0,1:T(8,128)(2,1)S(1)} collective-permute-done((bf16[256,1024]{0,1:T(8,128)(2,1)S(1)}, bf16[256,1024]{0,1:T(8,128)(2,1)S(1)}, u32[]{:S(2)}, u32[]{:S(2)}) %collective-permute-start.18) | collective-permute-done | bytes 524320 | tf_op jit(solution)/shard_map/ppermute | solution.py:18
  231.4 15.3 %collective-permute-done.19 = bf16[256,1024]{0,1:T(8,128)(2,1)S(1)} collective-permute-done((bf16[256,1024]{0,1:T(8,128)(2,1)S(1)}, bf16[256,1024]{0,1:T(8,128)(2,1)S(1)}, u32[]{:S(2)}, u32[]{:S(2)}) %collective-permute-start.19) | collective-permute-done | bytes 524320 | tf_op jit(solution)/shard_map/ppermute | solution.py:18
  252.1 5.3 collective-permute-done.21
  259.3 9.3 %collective-permute-done.22 = bf16[256,1024]{0,1:T(8,128)(2,1)S(1)} collective-permute-done((bf16[256,1024]{0,1:T(8,128)(2,1)S(1)}, bf16[256,1024]{0,1:T(8,128)(2,1)S(1)}, u32[]{:S(2)}, u32[]{:S(2)}) %collective-permute-start.22) | collective-permute-done | bytes 524320 | tf_op jit(solution)/shard_map/ppermute | solution.py:18
  270.6 9.4 %collective-permute-done.23 = bf16[256,1024]{0,1:T(8,128)(2,1)S(1)} collective-permute-done((bf16[256,1024]{0,1:T(8,128)(2,1)S(1)}, bf16[256,1024]{0,1:T(8,128)(2,1)S(1)}, u32[]{:S(2)}, u32[]{:S(2)}) %collective-permute-start.23) | collective-permute-done | bytes 524320 | tf_op jit(solution)/shard_map/ppermute | solution.py:18
  281.9 9.2 %collective-permute-done.24 = bf16[256,1024]{0,1:T(8,128)(2,1)S(1)} collective-permute-done((bf16[256,1024]{0,1:T(8,128)(2,1)S(1)}, bf16[256,1024]{0,1:T(8,128)(2,1)S(1)}, u32[]{:S(2)}, u32[]{:S(2)}) %collective-permute-start.24) | collective-permute-done | bytes 524320 | tf_op jit(solution)/shard_map/ppermute | solution.py:18
  291.1 7.7 %collective-permute-start.29 = (bf16[256,1024]{0,1:T(8,128)(2,1)S(1)}, bf16[256,1024]{0,1:T(8,128)(2,1)S(1)}, u32[]{:S(2)}, u32[]{:S(2)}) collective-permute-start(bf16[256,1024]{0,1:T(8,128)(2,1)S(1)} %bitcast.59), channel_id=1, source_target_pairs={{14,0},{15,1},{16,2},{17,3},{18,4},{19,5},{20,6},{21,7},{22,8},{23... | collective-permute-start | bytes 1572872 | tf_op jit(solution)/shard_map/ppermute | solution.py:18
  298.8 5.1 collective-permute-done.25
  305.9 7.7 %collective-permute-done.26 = bf16[256,1024]{0,1:T(8,128)(2,1)S(1)} collective-permute-done((bf16[256,1024]{0,1:T(8,128)(2,1)S(1)}, bf16[256,1024]{0,1:T(8,128)(2,1)S(1)}, u32[]{:S(2)}, u32[]{:S(2)}) %collective-permute-start.26) | collective-permute-done | bytes 524320 | tf_op jit(solution)/shard_map/ppermute | solution.py:18
  316.3 41.8 %collective-permute-done.27 = bf16[256,1024]{0,1:T(8,128)(2,1)S(1)} collective-permute-done((bf16[256,1024]{0,1:T(8,128)(2,1)S(1)}, bf16[256,1024]{0,1:T(8,128)(2,1)S(1)}, u32[]{:S(2)}, u32[]{:S(2)}) %collective-permute-start.27) | collective-permute-done | bytes 524320 | tf_op jit(solution)/shard_map/ppermute | solution.py:18
  359.6 9.6 %collective-permute-done.31 = bf16[256,1024]{0,1:T(8,128)(2,1)S(1)} collective-permute-done((bf16[256,1024]{0,1:T(8,128)(2,1)S(1)}, bf16[256,1024]{0,1:T(8,128)(2,1)S(1)}, u32[]{:S(2)}, u32[]{:S(2)}) %collective-permute-start.31) | collective-permute-done | bytes 524320 | tf_op jit(solution)/shard_map/ppermute | solution.py:18
  373.3 11.5 %multiply_reduce_fusion.6 = (f32[256]{0:T(256)S(1)}, f32[256,8448]{0,1:T(8,128)S(1)}) fusion(f32[8448]{0:T(1024)S(1)} %get-tuple-element.29, s32[8448]{0:T(1024)S(1)} %get-tuple-element.30, s32[256]{0:T(256)S(1)} %dynamic_slice.15, f32[8448]{0:T(1024)S(1)} %add_rsqrt_fusion, f32[256]{0:T(256)S(1)} %add_rsqrt_fusion.1, ...), kind=kOutput, calls=%fused_computation.14 | convolution fusion | flops 4459462656 | bytes 26625280 | tf_op jit(solution)/shard_map/dot_general | solution.py:66
  391.8 7.6 %collective-permute-start.33 = (f32[10240]{0:T(1024)S(1)}, f32[10240]{0:T(1024)S(1)}, u32[]{:S(2)}, u32[]{:S(2)}) collective-permute-start(f32[10240]{0:T(1024)S(1)} %add_dynamic-update-slice_fusion.2), channel_id=1, source_target_pairs={{0,2},{1,3},{2,0},{3,1},{4,6},{5,7},{6,4},{7,5},{8,10},{9,11},{10,... | collective-permute-start | bytes 122888 | tf_op jit(solution)/shard_map/ppermute | solution.py:87
  401.4 5.5 collective-permute-done.34
  412.8 5.5 collective-permute-start.41
  418.3 6.5 %collective-permute-start.37 = (f32[6144]{0:T(1024)S(1)}, f32[6144]{0:T(1024)S(1)}, u32[]{:S(2)}, u32[]{:S(2)}) collective-permute-start(f32[6144]{0:T(1024)S(1)} %get-tuple-element.25), channel_id=1, source_target_pairs={{16,0},{24,8},{32,16},{40,24},{48,32},{56,40},{64,48},{72,56},{80,... | collective-permute-start | bytes 73736 | tf_op jit(solution)/shard_map/ppermute | solution.py:18
  432.2 5.6 collective-permute-done.42
  437.9 5.7 multiply_reduce_fusion.4
  454.6 5.0 collective-permute-done.45
  459.6 4.5 collective-permute-start.46
  470.0 7.9 %collective-permute-start.48 = (f32[6144]{0:T(1024)S(1)}, f32[6144]{0:T(1024)S(1)}, u32[]{:S(2)}, u32[]{:S(2)}) collective-permute-start(f32[6144]{0:T(1024)S(1)} %get-tuple-element.17), channel_id=1, source_target_pairs={{16,0},{24,8},{32,16},{40,24},{48,32},{56,40},{64,48},{72,56},{80,... | collective-permute-start | bytes 73736 | tf_op jit(solution)/shard_map/ppermute | solution.py:18
  485.2 5.5 collective-permute-done.53
  490.8 5.7 multiply_reduce_fusion.2
  507.5 5.0 collective-permute-done.56
  512.5 4.6 collective-permute-start.57
  523.0 7.2 %collective-permute-start.59 = (f32[6144]{0:T(1024)S(1)}, f32[6144]{0:T(1024)S(1)}, u32[]{:S(2)}, u32[]{:S(2)}) collective-permute-start(f32[6144]{0:T(1024)S(1)} %get-tuple-element.9), channel_id=1, source_target_pairs={{16,0},{24,8},{32,16},{40,24},{48,32},{56,40},{64,48},{72,56},{80,... | collective-permute-start | bytes 73736 | tf_op jit(solution)/shard_map/ppermute | solution.py:18
  537.6 5.5 collective-permute-done.64
  543.2 6.0 %multiply_reduce_fusion.7 = f32[256]{0:T(256)S(1)} fusion(f32[256,8448]{0,1:T(8,128)} %copy-done, f32[8448]{0:T(1024)S(1)} %fusion.38), kind=kLoop, calls=%fused_computation.17 | loop fusion | flops 4325120 | bytes 8685568 | tf_op jit(solution)/shard_map/reduce_sum | solution.py:113
  549.2 12.8 %fusion.11 = bf16[32,8,8,128]{3,2,1,0:T(8,128)(2,1)S(1)} fusion(bf16[8448,1024]{0,1:T(8,128)(2,1)} %copy-done.1, f32[256,8448]{0,1:T(8,128)} %copy-done, f32[256]{0:T(256)S(1)} %multiply_reduce_fusion.7, f32[8448]{0:T(1024)S(1)} %fusion.38), kind=kOutput, calls=%fused_computation.22 | convolution fusion | flops 4435935232 | bytes 26511360 | tf_op jit(solution)/shard_map/dot_general | solution.py:116
  566.9 9.7 %all-to-all-done.2 = bf16[256,8,128]{2,0,1:T(8,128)(2,1)S(1)} async-done(((bf16[256,8,128]{2,0,1:T(8,128)(2,1)}), bf16[256,8,128]{2,0,1:T(8,128)(2,1)S(1)}, u32[]{:S(2)}, u32[]{:S(2)}) %all-to-all-start.2) | async-done | bytes 524320 | tf_op jit(solution)/shard_map/all_to_all | solution.py:117
  (184 shorter events, 149.5 us)
Async XLA Ops:
  0.6 15.6 %all-to-all-start = ((bf16[8,256,128]{2,1,0:T(8,128)(2,1)}), bf16[8,256,128]{2,1,0:T(8,128)(2,1)S(1)}, u32[]{:S(2)}, u32[]{:S(2)}) async-start(bf16[8,256,128]{2,1,0:T(8,128)(2,1)} %bitcast.64), calls=%async_computation | async-start | bytes 1048576 | tf_op jit(solution)/shard_map/all_to_all | solution.py:31
  16.3 19.0 %all-to-all-start.1 = ((bf16[8,256,128]{2,1,0:T(8,128)(2,1)}), bf16[8,256,128]{2,1,0:T(8,128)(2,1)S(1)}, u32[]{:S(2)}, u32[]{:S(2)}) async-start(bf16[8,256,128]{2,1,0:T(8,128)(2,1)} %bitcast.65), calls=%async_computation.1 | async-start | bytes 1048576 | tf_op jit(solution)/shard_map/all_to_all | solution.py:30
  20.9 19.1 %collective-permute-start = (bf16[256,1024]{0,1:T(8,128)(2,1)S(1)}, bf16[256,1024]{0,1:T(8,128)(2,1)S(1)}, u32[]{:S(2)}, u32[]{:S(2)}) collective-permute-start(bf16[256,1024]{0,1:T(8,128)(2,1)S(1)} %bitcast.29), channel_id=1, source_target_pairs={{0,16},{1,17},{2,18},{3,19},{4,20},{5,21},{6,22},{7,23},{8,24},{9,... | collective-permute-start | bytes 1572872 | tf_op jit(solution)/shard_map/ppermute | solution.py:18
  24.9 29.3 %collective-permute-start.1 = (bf16[256,1024]{0,1:T(8,128)(2,1)S(1)}, bf16[256,1024]{0,1:T(8,128)(2,1)S(1)}, u32[]{:S(2)}, u32[]{:S(2)}) collective-permute-start(bf16[256,1024]{0,1:T(8,128)(2,1)S(1)} %bitcast.30), channel_id=1, source_target_pairs={{0,15},{1,16},{2,17},{3,18},{4,19},{5,20},{6,21},{7,22},{8,23},{9,... | collective-permute-start | bytes 1572872 | tf_op jit(solution)/shard_map/ppermute | solution.py:18
  29.5 37.6 %collective-permute-start.2 = (bf16[256,1024]{0,1:T(8,128)(2,1)S(1)}, bf16[256,1024]{0,1:T(8,128)(2,1)}, u32[]{:S(2)}, u32[]{:S(2)}) collective-permute-start(bf16[256,1024]{0,1:T(8,128)(2,1)S(1)} %bitcast.31), channel_id=1, source_target_pairs={{0,14},{1,15},{2,16},{3,17},{4,18},{5,19},{6,20},{7,21},{8,22},{9,... | collective-permute-start | bytes 1572872 | tf_op jit(solution)/shard_map/ppermute | solution.py:18
  31.4 46.9 %collective-permute-start.3 = (bf16[256,1024]{0,1:T(8,128)(2,1)S(1)}, bf16[256,1024]{0,1:T(8,128)(2,1)}, u32[]{:S(2)}, u32[]{:S(2)}) collective-permute-start(bf16[256,1024]{0,1:T(8,128)(2,1)S(1)} %bitcast.32), channel_id=1, source_target_pairs={{0,13},{1,14},{2,15},{3,16},{4,17},{5,18},{6,19},{7,20},{8,21},{9,... | collective-permute-start | bytes 1572872 | tf_op jit(solution)/shard_map/ppermute | solution.py:18
  33.3 56.2 %collective-permute-start.4 = (bf16[256,1024]{0,1:T(8,128)(2,1)S(1)}, bf16[256,1024]{0,1:T(8,128)(2,1)S(1)}, u32[]{:S(2)}, u32[]{:S(2)}) collective-permute-start(bf16[256,1024]{0,1:T(8,128)(2,1)S(1)} %bitcast.33), channel_id=1, source_target_pairs={{0,12},{1,13},{2,14},{3,15},{4,16},{5,17},{6,18},{7,19},{8,20},{9,... | collective-permute-start | bytes 1572872 | tf_op jit(solution)/shard_map/ppermute | solution.py:18
  40.0 61.0 %collective-permute-start.5 = (bf16[256,1024]{0,1:T(8,128)(2,1)S(1)}, bf16[256,1024]{0,1:T(8,128)(2,1)S(1)}, u32[]{:S(2)}, u32[]{:S(2)}) collective-permute-start(bf16[256,1024]{0,1:T(8,128)(2,1)S(1)} %bitcast.34), channel_id=1, source_target_pairs={{0,11},{1,12},{2,13},{3,14},{4,15},{5,16},{6,17},{7,18},{8,19},{9,... | collective-permute-start | bytes 1572872 | tf_op jit(solution)/shard_map/ppermute | solution.py:18
  54.2 57.9 %collective-permute-start.6 = (bf16[256,1024]{0,1:T(8,128)(2,1)S(1)}, bf16[256,1024]{0,1:T(8,128)(2,1)S(1)}, u32[]{:S(2)}, u32[]{:S(2)}) collective-permute-start(bf16[256,1024]{0,1:T(8,128)(2,1)S(1)} %bitcast.35), channel_id=1, source_target_pairs={{0,10},{1,11},{2,12},{3,13},{4,14},{5,15},{6,16},{7,17},{8,18},{9,... | collective-permute-start | bytes 1572872 | tf_op jit(solution)/shard_map/ppermute | solution.py:18
  67.1 56.3 %collective-permute-start.7 = (bf16[256,1024]{0,1:T(8,128)(2,1)S(1)}, bf16[256,1024]{0,1:T(8,128)(2,1)S(1)}, u32[]{:S(2)}, u32[]{:S(2)}) collective-permute-start(bf16[256,1024]{0,1:T(8,128)(2,1)S(1)} %bitcast.36), channel_id=1, source_target_pairs={{0,9},{1,10},{2,11},{3,12},{4,13},{5,14},{6,15},{7,16},{8,17},{9,1... | collective-permute-start | bytes 1572872 | tf_op jit(solution)/shard_map/ppermute | solution.py:18
  78.3 56.3 %collective-permute-start.8 = (bf16[256,1024]{0,1:T(8,128)(2,1)S(1)}, bf16[256,1024]{0,1:T(8,128)(2,1)S(1)}, u32[]{:S(2)}, u32[]{:S(2)}) collective-permute-start(bf16[256,1024]{0,1:T(8,128)(2,1)S(1)} %bitcast.37), channel_id=1, source_target_pairs={{0,8},{1,9},{2,10},{3,11},{4,12},{5,13},{6,14},{7,15},{8,16},{9,17... | collective-permute-start | bytes 1572872 | tf_op jit(solution)/shard_map/ppermute | solution.py:18
  89.5 47.1 %collective-permute-start.9 = (bf16[256,1024]{0,1:T(8,128)(2,1)S(1)}, bf16[256,1024]{0,1:T(8,128)(2,1)S(1)}, u32[]{:S(2)}, u32[]{:S(2)}) collective-permute-start(bf16[256,1024]{0,1:T(8,128)(2,1)S(1)} %bitcast.38), channel_id=1, source_target_pairs={{0,7},{1,8},{2,9},{3,10},{4,11},{5,12},{6,13},{7,14},{8,15},{9,16}... | collective-permute-start | bytes 1572872 | tf_op jit(solution)/shard_map/ppermute | solution.py:18
  100.9 54.4 %collective-permute-start.10 = (bf16[256,1024]{0,1:T(8,128)(2,1)S(1)}, bf16[256,1024]{0,1:T(8,128)(2,1)S(1)}, u32[]{:S(2)}, u32[]{:S(2)}) collective-permute-start(bf16[256,1024]{0,1:T(8,128)(2,1)S(1)} %bitcast.39), channel_id=1, source_target_pairs={{0,6},{1,7},{2,8},{3,9},{4,10},{5,11},{6,12},{7,13},{8,14},{9,15},... | collective-permute-start | bytes 1572872 | tf_op jit(solution)/shard_map/ppermute | solution.py:18
  112.2 54.7 %collective-permute-start.11 = (bf16[256,1024]{0,1:T(8,128)(2,1)S(1)}, bf16[256,1024]{0,1:T(8,128)(2,1)S(1)}, u32[]{:S(2)}, u32[]{:S(2)}) collective-permute-start(bf16[256,1024]{0,1:T(8,128)(2,1)S(1)} %bitcast.40), channel_id=1, source_target_pairs={{0,5},{1,6},{2,7},{3,8},{4,9},{5,10},{6,11},{7,12},{8,13},{9,14},{... | collective-permute-start | bytes 1572872 | tf_op jit(solution)/shard_map/ppermute | solution.py:18
  123.4 54.9 %collective-permute-start.12 = (bf16[256,1024]{0,1:T(8,128)(2,1)S(1)}, bf16[256,1024]{0,1:T(8,128)(2,1)S(1)}, u32[]{:S(2)}, u32[]{:S(2)}) collective-permute-start(bf16[256,1024]{0,1:T(8,128)(2,1)S(1)} %bitcast.41), channel_id=1, source_target_pairs={{0,4},{1,5},{2,6},{3,7},{4,8},{5,9},{6,10},{7,11},{8,12},{9,13},{1... | collective-permute-start | bytes 1572872 | tf_op jit(solution)/shard_map/ppermute | solution.py:18
  134.6 54.4 %collective-permute-start.13 = (bf16[256,1024]{0,1:T(8,128)(2,1)S(1)}, bf16[256,1024]{0,1:T(8,128)(2,1)S(1)}, u32[]{:S(2)}, u32[]{:S(2)}) collective-permute-start(bf16[256,1024]{0,1:T(8,128)(2,1)S(1)} %bitcast.42), channel_id=1, source_target_pairs={{0,3},{1,4},{2,5},{3,6},{4,7},{5,8},{6,9},{7,10},{8,11},{9,12},{10... | collective-permute-start | bytes 1572872 | tf_op jit(solution)/shard_map/ppermute | solution.py:18
  136.6 67.5 %collective-permute-start.14 = (bf16[256,1024]{0,1:T(8,128)(2,1)S(1)}, bf16[256,1024]{0,1:T(8,128)(2,1)S(1)}, u32[]{:S(2)}, u32[]{:S(2)}) collective-permute-start(bf16[256,1024]{0,1:T(8,128)(2,1)S(1)} %bitcast.43), channel_id=1, source_target_pairs={{0,2},{1,3},{2,4},{3,5},{4,6},{5,7},{6,8},{7,9},{8,10},{9,11},{10,... | collective-permute-start | bytes 1572872 | tf_op jit(solution)/shard_map/ppermute | solution.py:18
  155.3 58.4 %collective-permute-start.15 = (bf16[256,1024]{0,1:T(8,128)(2,1)S(1)}, bf16[256,1024]{0,1:T(8,128)(2,1)S(1)}, u32[]{:S(2)}, u32[]{:S(2)}) collective-permute-start(bf16[256,1024]{0,1:T(8,128)(2,1)S(1)} %bitcast.44), channel_id=1, source_target_pairs={{0,1},{1,2},{2,3},{3,4},{4,5},{5,6},{6,7},{7,8},{8,9},{9,10},{10,1... | collective-permute-start | bytes 1572872 | tf_op jit(solution)/shard_map/ppermute | solution.py:18
  166.8 48.9 %collective-permute-start.16 = (bf16[256,1024]{0,1:T(8,128)(2,1)S(1)}, bf16[256,1024]{0,1:T(8,128)(2,1)S(1)}, u32[]{:S(2)}, u32[]{:S(2)}) collective-permute-start(bf16[256,1024]{0,1:T(8,128)(2,1)S(1)} %bitcast.45), channel_id=1, source_target_pairs={{1,0},{2,1},{3,2},{4,3},{5,4},{6,5},{7,6},{8,7},{9,8},{10,9},{11,1... | collective-permute-start | bytes 1572872 | tf_op jit(solution)/shard_map/ppermute | solution.py:18
  178.3 39.4 %collective-permute-start.17 = (bf16[256,1024]{0,1:T(8,128)(2,1)S(1)}, bf16[256,1024]{0,1:T(8,128)(2,1)S(1)}, u32[]{:S(2)}, u32[]{:S(2)}) collective-permute-start(bf16[256,1024]{0,1:T(8,128)(2,1)S(1)} %bitcast.46), channel_id=1, source_target_pairs={{2,0},{3,1},{4,2},{5,3},{6,4},{7,5},{8,6},{9,7},{10,8},{11,9},{12,... | collective-permute-start | bytes 1572872 | tf_op jit(solution)/shard_map/ppermute | solution.py:18
  189.0 40.4 %collective-permute-start.18 = (bf16[256,1024]{0,1:T(8,128)(2,1)S(1)}, bf16[256,1024]{0,1:T(8,128)(2,1)S(1)}, u32[]{:S(2)}, u32[]{:S(2)}) collective-permute-start(bf16[256,1024]{0,1:T(8,128)(2,1)S(1)} %bitcast.47), channel_id=1, source_target_pairs={{3,0},{4,1},{5,2},{6,3},{7,4},{8,5},{9,6},{10,7},{11,8},{12,9},{13... | collective-permute-start | bytes 1572872 | tf_op jit(solution)/shard_map/ppermute | solution.py:18
  204.1 42.5 %collective-permute-start.19 = (bf16[256,1024]{0,1:T(8,128)(2,1)S(1)}, bf16[256,1024]{0,1:T(8,128)(2,1)S(1)}, u32[]{:S(2)}, u32[]{:S(2)}) collective-permute-start(bf16[256,1024]{0,1:T(8,128)(2,1)S(1)} %bitcast.48), channel_id=1, source_target_pairs={{4,0},{5,1},{6,2},{7,3},{8,4},{9,5},{10,6},{11,7},{12,8},{13,9},{1... | collective-permute-start | bytes 1572872 | tf_op jit(solution)/shard_map/ppermute | solution.py:18
  213.7 36.4 %collective-permute-start.20 = (bf16[256,1024]{0,1:T(8,128)(2,1)S(1)}, bf16[256,1024]{0,1:T(8,128)(2,1)S(1)}, u32[]{:S(2)}, u32[]{:S(2)}) collective-permute-start(bf16[256,1024]{0,1:T(8,128)(2,1)S(1)} %bitcast.49), channel_id=1, source_target_pairs={{5,0},{6,1},{7,2},{8,3},{9,4},{10,5},{11,6},{12,7},{13,8},{14,9},{... | collective-permute-start | bytes 1572872 | tf_op jit(solution)/shard_map/ppermute | solution.py:18
  215.8 41.6 %collective-permute-start.21 = (bf16[256,1024]{0,1:T(8,128)(2,1)S(1)}, bf16[256,1024]{0,1:T(8,128)(2,1)S(1)}, u32[]{:S(2)}, u32[]{:S(2)}) collective-permute-start(bf16[256,1024]{0,1:T(8,128)(2,1)S(1)} %bitcast.51), channel_id=1, source_target_pairs={{6,0},{7,1},{8,2},{9,3},{10,4},{11,5},{12,6},{13,7},{14,8},{15,9},... | collective-permute-start | bytes 1572872 | tf_op jit(solution)/shard_map/ppermute | solution.py:18
  217.7 50.9 %collective-permute-start.22 = (bf16[256,1024]{0,1:T(8,128)(2,1)S(1)}, bf16[256,1024]{0,1:T(8,128)(2,1)S(1)}, u32[]{:S(2)}, u32[]{:S(2)}) collective-permute-start(bf16[256,1024]{0,1:T(8,128)(2,1)S(1)} %bitcast.52), channel_id=1, source_target_pairs={{7,0},{8,1},{9,2},{10,3},{11,4},{12,5},{13,6},{14,7},{15,8},{16,9}... | collective-permute-start | bytes 1572872 | tf_op jit(solution)/shard_map/ppermute | solution.py:18
  229.4 50.5 %collective-permute-start.23 = (bf16[256,1024]{0,1:T(8,128)(2,1)S(1)}, bf16[256,1024]{0,1:T(8,128)(2,1)S(1)}, u32[]{:S(2)}, u32[]{:S(2)}) collective-permute-start(bf16[256,1024]{0,1:T(8,128)(2,1)S(1)} %bitcast.53), channel_id=1, source_target_pairs={{8,0},{9,1},{10,2},{11,3},{12,4},{13,5},{14,6},{15,7},{16,8},{17,9... | collective-permute-start | bytes 1572872 | tf_op jit(solution)/shard_map/ppermute | solution.py:18
  246.6 44.4 %collective-permute-start.24 = (bf16[256,1024]{0,1:T(8,128)(2,1)S(1)}, bf16[256,1024]{0,1:T(8,128)(2,1)S(1)}, u32[]{:S(2)}, u32[]{:S(2)}) collective-permute-start(bf16[256,1024]{0,1:T(8,128)(2,1)S(1)} %bitcast.54), channel_id=1, source_target_pairs={{9,0},{10,1},{11,2},{12,3},{13,4},{14,5},{15,6},{16,7},{17,8},{18,... | collective-permute-start | bytes 1572872 | tf_op jit(solution)/shard_map/ppermute | solution.py:18
  250.1 53.8 %collective-permute-start.25 = (bf16[256,1024]{0,1:T(8,128)(2,1)S(1)}, bf16[256,1024]{0,1:T(8,128)(2,1)S(1)}, u32[]{:S(2)}, u32[]{:S(2)}) collective-permute-start(bf16[256,1024]{0,1:T(8,128)(2,1)S(1)} %bitcast.55), channel_id=1, source_target_pairs={{10,0},{11,1},{12,2},{13,3},{14,4},{15,5},{16,6},{17,7},{18,8},{19... | collective-permute-start | bytes 1572872 | tf_op jit(solution)/shard_map/ppermute | solution.py:18
  257.4 56.2 %collective-permute-start.26 = (bf16[256,1024]{0,1:T(8,128)(2,1)S(1)}, bf16[256,1024]{0,1:T(8,128)(2,1)S(1)}, u32[]{:S(2)}, u32[]{:S(2)}) collective-permute-start(bf16[256,1024]{0,1:T(8,128)(2,1)S(1)} %bitcast.56), channel_id=1, source_target_pairs={{11,0},{12,1},{13,2},{14,3},{15,4},{16,5},{17,6},{18,7},{19,8},{20... | collective-permute-start | bytes 1572872 | tf_op jit(solution)/shard_map/ppermute | solution.py:18
  268.6 89.5 %collective-permute-start.27 = (bf16[256,1024]{0,1:T(8,128)(2,1)S(1)}, bf16[256,1024]{0,1:T(8,128)(2,1)S(1)}, u32[]{:S(2)}, u32[]{:S(2)}) collective-permute-start(bf16[256,1024]{0,1:T(8,128)(2,1)S(1)} %bitcast.57), channel_id=1, source_target_pairs={{12,0},{13,1},{14,2},{15,3},{16,4},{17,5},{18,6},{19,7},{20,8},{21... | collective-permute-start | bytes 1572872 | tf_op jit(solution)/shard_map/ppermute | solution.py:18
  280.0 79.5 %collective-permute-start.28 = (bf16[256,1024]{0,1:T(8,128)(2,1)S(1)}, bf16[256,1024]{0,1:T(8,128)(2,1)S(1)}, u32[]{:S(2)}, u32[]{:S(2)}) collective-permute-start(bf16[256,1024]{0,1:T(8,128)(2,1)S(1)} %bitcast.58), channel_id=1, source_target_pairs={{13,0},{14,1},{15,2},{16,3},{17,4},{18,5},{19,6},{20,7},{21,8},{22... | collective-permute-start | bytes 1572872 | tf_op jit(solution)/shard_map/ppermute | solution.py:18
  291.1 68.4 %collective-permute-start.29 = (bf16[256,1024]{0,1:T(8,128)(2,1)S(1)}, bf16[256,1024]{0,1:T(8,128)(2,1)S(1)}, u32[]{:S(2)}, u32[]{:S(2)}) collective-permute-start(bf16[256,1024]{0,1:T(8,128)(2,1)S(1)} %bitcast.59), channel_id=1, source_target_pairs={{14,0},{15,1},{16,2},{17,3},{18,4},{19,5},{20,6},{21,7},{22,8},{23... | collective-permute-start | bytes 1572872 | tf_op jit(solution)/shard_map/ppermute | solution.py:18
  303.9 55.7 %collective-permute-start.30 = (bf16[256,1024]{0,1:T(8,128)(2,1)S(1)}, bf16[256,1024]{0,1:T(8,128)(2,1)S(1)}, u32[]{:S(2)}, u32[]{:S(2)}) collective-permute-start(bf16[256,1024]{0,1:T(8,128)(2,1)S(1)} %bitcast.60), channel_id=1, source_target_pairs={{15,0},{16,1},{17,2},{18,3},{19,4},{20,5},{21,6},{22,7},{23,8},{24... | collective-permute-start | bytes 1572872 | tf_op jit(solution)/shard_map/ppermute | solution.py:18
  313.5 55.7 %collective-permute-start.31 = (bf16[256,1024]{0,1:T(8,128)(2,1)S(1)}, bf16[256,1024]{0,1:T(8,128)(2,1)S(1)}, u32[]{:S(2)}, u32[]{:S(2)}) collective-permute-start(bf16[256,1024]{0,1:T(8,128)(2,1)S(1)} %bitcast.61), channel_id=1, source_target_pairs={{16,0},{17,1},{18,2},{19,3},{20,4},{21,5},{22,6},{23,7},{24,8},{25... | collective-permute-start | bytes 1572872 | tf_op jit(solution)/shard_map/ppermute | solution.py:18
  406.9 22.7 %collective-permute-start.35 = (f32[8192]{0:T(1024)S(1)}, f32[8192]{0:T(1024)S(1)}, u32[]{:S(2)}, u32[]{:S(2)}) collective-permute-start(f32[8192]{0:T(1024)S(1)} %get-tuple-element.18), channel_id=1, source_target_pairs={{8,0},{16,8},{24,16},{32,24},{40,32},{48,40},{56,48},{64,56},{72,6... | collective-permute-start | bytes 98312 | tf_op jit(solution)/shard_map/ppermute | solution.py:18
  408.8 22.0 %collective-permute-start.36 = (f32[8192]{0:T(1024)S(1)}, f32[8192]{0:T(1024)S(1)}, u32[]{:S(2)}, u32[]{:S(2)}) collective-permute-start(f32[8192]{0:T(1024)S(1)} %get-tuple-element.19), channel_id=1, source_target_pairs={{0,8},{8,16},{16,24},{24,32},{32,40},{40,48},{48,56},{56,64},{64,7... | collective-permute-start | bytes 98312 | tf_op jit(solution)/shard_map/ppermute | solution.py:18
  412.8 14.0 %collective-permute-start.41 = (f32[2048]{0:T(1024)S(1)}, f32[2048]{0:T(1024)S(1)}, u32[]{:S(2)}, u32[]{:S(2)}) collective-permute-start(f32[2048]{0:T(1024)S(1)} %get-tuple-element.21), channel_id=1, source_target_pairs={{32,0},{40,8},{48,16},{56,24},{64,32},{72,40},{80,48},{88,56},{96,... | collective-permute-start | bytes 24584 | tf_op jit(solution)/shard_map/ppermute | solution.py:18
  418.3 19.5 %collective-permute-start.37 = (f32[6144]{0:T(1024)S(1)}, f32[6144]{0:T(1024)S(1)}, u32[]{:S(2)}, u32[]{:S(2)}) collective-permute-start(f32[6144]{0:T(1024)S(1)} %get-tuple-element.25), channel_id=1, source_target_pairs={{16,0},{24,8},{32,16},{40,24},{48,32},{56,40},{64,48},{72,56},{80,... | collective-permute-start | bytes 73736 | tf_op jit(solution)/shard_map/ppermute | solution.py:18
  424.8 12.9 %collective-permute-start.38 = (f32[6144]{0:T(1024)S(1)}, f32[6144]{0:T(1024)S(1)}, u32[]{:S(2)}, u32[]{:S(2)}) collective-permute-start(f32[6144]{0:T(1024)S(1)} %get-tuple-element.24), channel_id=1, source_target_pairs={{0,16},{8,24},{16,32},{24,40},{32,48},{40,56},{48,64},{56,72},{64,... | collective-permute-start | bytes 73736 | tf_op jit(solution)/shard_map/ppermute | solution.py:18
  459.6 23.0 %collective-permute-start.46 = (f32[8192]{0:T(1024)S(1)}, f32[8192]{0:T(1024)S(1)}, u32[]{:S(2)}, u32[]{:S(2)}) collective-permute-start(f32[8192]{0:T(1024)S(1)} %get-tuple-element.10), channel_id=1, source_target_pairs={{8,0},{16,8},{24,16},{32,24},{40,32},{48,40},{56,48},{64,56},{72,6... | collective-permute-start | bytes 98312 | tf_op jit(solution)/shard_map/ppermute | solution.py:18
  464.1 19.8 %collective-permute-start.47 = (f32[8192]{0:T(1024)S(1)}, f32[8192]{0:T(1024)S(1)}, u32[]{:S(2)}, u32[]{:S(2)}) collective-permute-start(f32[8192]{0:T(1024)S(1)} %get-tuple-element.11), channel_id=1, source_target_pairs={{0,8},{8,16},{16,24},{24,32},{32,40},{40,48},{48,56},{56,64},{64,7... | collective-permute-start | bytes 98312 | tf_op jit(solution)/shard_map/ppermute | solution.py:18
  466.2 13.6 %collective-permute-start.52 = (f32[2048]{0:T(1024)S(1)}, f32[2048]{0:T(1024)S(1)}, u32[]{:S(2)}, u32[]{:S(2)}) collective-permute-start(f32[2048]{0:T(1024)S(1)} %get-tuple-element.13), channel_id=1, source_target_pairs={{32,0},{40,8},{48,16},{56,24},{64,32},{72,40},{80,48},{88,56},{96,... | collective-permute-start | bytes 24584 | tf_op jit(solution)/shard_map/ppermute | solution.py:18
  470.0 20.7 %collective-permute-start.48 = (f32[6144]{0:T(1024)S(1)}, f32[6144]{0:T(1024)S(1)}, u32[]{:S(2)}, u32[]{:S(2)}) collective-permute-start(f32[6144]{0:T(1024)S(1)} %get-tuple-element.17), channel_id=1, source_target_pairs={{16,0},{24,8},{32,16},{40,24},{48,32},{56,40},{64,48},{72,56},{80,... | collective-permute-start | bytes 73736 | tf_op jit(solution)/shard_map/ppermute | solution.py:18
  512.5 22.4 %collective-permute-start.57 = (f32[8192]{0:T(1024)S(1)}, f32[8192]{0:T(1024)S(1)}, u32[]{:S(2)}, u32[]{:S(2)}) collective-permute-start(f32[8192]{0:T(1024)S(1)} %get-tuple-element.2), channel_id=1, source_target_pairs={{8,0},{16,8},{24,16},{32,24},{40,32},{48,40},{56,48},{64,56},{72,6... | collective-permute-start | bytes 98312 | tf_op jit(solution)/shard_map/ppermute | solution.py:18
  517.1 19.1 %collective-permute-start.58 = (f32[8192]{0:T(1024)S(1)}, f32[8192]{0:T(1024)S(1)}, u32[]{:S(2)}, u32[]{:S(2)}) collective-permute-start(f32[8192]{0:T(1024)S(1)} %get-tuple-element.3), channel_id=1, source_target_pairs={{0,8},{8,16},{16,24},{24,32},{32,40},{40,48},{48,56},{56,64},{64,7... | collective-permute-start | bytes 98312 | tf_op jit(solution)/shard_map/ppermute | solution.py:18
  519.2 12.9 %collective-permute-start.63 = (f32[2048]{0:T(1024)S(1)}, f32[2048]{0:T(1024)S(1)}, u32[]{:S(2)}, u32[]{:S(2)}) collective-permute-start(f32[2048]{0:T(1024)S(1)} %get-tuple-element.5), channel_id=1, source_target_pairs={{32,0},{40,8},{48,16},{56,24},{64,32},{72,40},{80,48},{88,56},{96,... | collective-permute-start | bytes 24584 | tf_op jit(solution)/shard_map/ppermute | solution.py:18
  523.0 20.1 %collective-permute-start.59 = (f32[6144]{0:T(1024)S(1)}, f32[6144]{0:T(1024)S(1)}, u32[]{:S(2)}, u32[]{:S(2)}) collective-permute-start(f32[6144]{0:T(1024)S(1)} %get-tuple-element.9), channel_id=1, source_target_pairs={{16,0},{24,8},{32,16},{40,24},{48,32},{56,40},{64,48},{72,56},{80,... | collective-permute-start | bytes 73736 | tf_op jit(solution)/shard_map/ppermute | solution.py:18
  562.8 13.7 %all-to-all-start.2 = ((bf16[256,8,128]{2,0,1:T(8,128)(2,1)}), bf16[256,8,128]{2,0,1:T(8,128)(2,1)S(1)}, u32[]{:S(2)}, u32[]{:S(2)}) async-start(bf16[256,8,128]{2,0,1:T(8,128)(2,1)} %bitcast.27), calls=%async_computation.2 | async-start | bytes 1048576 | tf_op jit(solution)/shard_map/all_to_all | solution.py:117
  (22 other events, 160.3 us)
